TPU v7x, 256 devices: a whole 4x4x8 slice. The times are simulated.
256 devices in a mesh: dp: 8 (over x, z_hi), tensor: 32 (over y, z_lo, core).
Axes of the slice: x: 4, y: 4, z: 8 (z_hi: 2, z_lo: 4; z = z_hi * 4 + z_lo), core: 2. Of those that a mesh axis runs over, the one named last changes fastest.
Arguments:
- tokens: bfloat16 [8, 4096, 1280], P('dp', 'tensor'), may hold values from -6 to 6
- segment_ids: int32 [8, 4096], P('dp', 'tensor'), may hold values from 0 to 3, never falling along the last dimension, each value on 1 to 2048 neighbouring positions
- pack_of_group: int32 [32], replicated, may hold values from 0 to 31, each once
- w_qkv: bfloat16 [1280, 1920], replicated, may hold values from -0.11320094 to 0.11320094
- qk_gain: float32 [640], replicated, may hold values from 0.5 to 7
- w_out: bfloat16 [640, 1280], replicated, may hold values from -0.25 to 0.25
- alpha_attn: float32 [1280], replicated, may hold values from 0.05 to 0.6
- w_up: bfloat16 [1280, 5120], P(None, 'dp'), may hold values from -0.15625 to 0.15625
- w_gate: bfloat16 [1280, 5120], P(None, 'dp'), may hold values from -0.15625 to 0.15625
- up_gain: float32 [5120], P('dp'), may hold values from 0.5 to 2
- gate_gain: float32 [5120], P('dp'), may hold values from 0.5 to 2
- w_down: bfloat16 [5120, 1280], P('dp'), may hold values from -0.078125 to 0.078125
- alpha_mlp: float32 [1280], replicated, may hold values from 0.05 to 0.6
- w_vocab: bfloat16 [1280, 32000], P(None, ('dp', 'tensor')), may hold values from -0.15625 to 0.15625
- logit_gain: bfloat16 [32000], P(('dp', 'tensor')), may hold values from 1 to 10
Outputs:
- result_rows: bfloat16 [8, 4096, 1280], P('dp', 'tensor')
- request_norm: float32 [32], replicated
- max_logit: float32 [32], replicated
Inputs may be any that keep to these rules, and one draw needn't show every extreme that they name: `segment_ids`: within a pack the request numbers never fall, every request 0 to 3 has one or more tokens, and one request has exactly 2048 tokens.
All inputs are finite; a program needn't handle non-finite values.
Results may differ from a plain program's by a relative error of at most 0.013.
Values may be sent and summed in bfloat16 or wider, within the bound.
No kernel may reach another device: no remote copies, remote signals or barrier semaphores. Data moves between devices by JAX's collectives and lax.ppermute only.
A program may use at most 128 MiB of HBM per device.

v0:
```python
import math

import jax
import jax.numpy as jnp
from jax import lax
from jax.sharding import PartitionSpec as P

HEADS = 10
HD = 64
REQS = 4


EPSILON = 1e-06
NEGATIVE = -1e30


def normalize(values):
    return values * lax.rsqrt(jnp.mean(values * values, axis=-1, keepdims=True) + EPSILON)


def head_norm(values, qk_gain):
    reshaped = values.reshape(values.shape[0], HEADS, HD)
    return (normalize(reshaped) * qk_gain.reshape(HEADS, HD)).astype(jnp.bfloat16)


def local(
    tokens,
    segment_ids,
    pack_of_group,
    w_qkv,
    qk_gain,
    w_out,
    alpha_attn,
    w_up,
    w_gate,
    up_gain,
    gate_gain,
    w_down,
    alpha_mlp,
    w_vocab,
    logit_gain,
):
    row_count = tokens.shape[1]
    head_width = HEADS * HD
    segments = segment_ids[0]
    tensor_index = lax.axis_index("tensor")
    positions = tensor_index * row_count + jnp.arange(row_count, dtype=jnp.int32)
    request_numbers = jnp.arange(REQS, dtype=jnp.int32)
    start_rows = normalize(tokens[0].astype(jnp.float32)).astype(jnp.bfloat16)
    projected = jnp.dot(start_rows, w_qkv, preferred_element_type=jnp.float32)
    queries = head_norm(projected[:, :head_width], qk_gain)
    key_rows = head_norm(projected[:, head_width : 2 * head_width], qk_gain).reshape(
        row_count, head_width
    )
    value_rows = projected[:, 2 * head_width :].astype(jnp.bfloat16)
    score_scale = 1.0 / math.sqrt(HD)
    offset = jnp.int32(0)
    state_now = (
        jnp.full((HEADS, row_count), NEGATIVE, jnp.float32),
        jnp.zeros((HEADS, row_count), jnp.float32),
        jnp.zeros((HEADS, row_count, HD), jnp.float32),
    )
    key_all = lax.all_gather(key_rows, "tensor", axis=0, tiled=True)
    value_all = lax.all_gather(value_rows, "tensor", axis=0, tiled=True)
    seg_all = lax.all_gather(segments, "tensor", axis=0, tiled=True)
    tally = jnp.sum((seg_all[:, None] == request_numbers[None, :]).astype(jnp.int32), axis=0)
    total_keys = key_all.shape[0]
    step_size = math.gcd(total_keys, 512)
    for begin in range(0, total_keys, step_size):
        key_part = key_all[begin : begin + step_size]
        value_part = value_all[begin : begin + step_size]
        seg_part = seg_all[begin : begin + step_size]
        key_pos = offset + begin + jnp.arange(step_size, dtype=jnp.int32)
        update_running_max, update_weight_sum, update_weighted = state_now
        key_count = key_part.shape[0]
        key_heads = key_part.reshape(key_count, HEADS, HD)
        value_heads = value_part.reshape(key_count, HEADS, HD)
        scores = (
            jnp.einsum("qhd,khd->hqk", queries, key_heads, preferred_element_type=jnp.float32)
            * score_scale
        )
        allowed = (seg_part[None, :] == segments[:, None]) & (
            key_pos[None, :] <= positions[:, None]
        )
        new_max = jnp.maximum(
            update_running_max, jnp.max(jnp.where(allowed[None], scores, NEGATIVE), axis=2)
        )
        weights = jnp.where(allowed[None], jnp.exp(scores - new_max[:, :, None]), 0.0)
        factor = jnp.exp(update_running_max - new_max)
        update_weight_sum = update_weight_sum * factor + jnp.sum(weights, axis=2)
        update_weighted = update_weighted * factor[:, :, None] + jnp.einsum(
            "hqk,khd->hqd",
            weights.astype(jnp.bfloat16),
            value_heads,
            preferred_element_type=jnp.float32,
        )
        state_now = (new_max, update_weight_sum, update_weighted)
    folded, tally = (state_now, tally)
    running_max, weight_sum, weighted = folded
    attended = (
        (weighted / weight_sum[:, :, None])
        .transpose(1, 0, 2)
        .reshape(row_count, head_width)
        .astype(jnp.bfloat16)
    )
    attn_rows = normalize(jnp.dot(attended, w_out, preferred_element_type=jnp.float32))
    residual_in = start_rows.astype(jnp.float32)
    mid_rows = normalize(residual_in + alpha_attn * (attn_rows - residual_in)).astype(jnp.bfloat16)
    received = lax.all_gather(mid_rows, "dp", axis=0, tiled=True)
    up_proj = jnp.dot(received, w_up, preferred_element_type=jnp.float32) * up_gain
    gate_proj = jnp.dot(received, w_gate, preferred_element_type=jnp.float32) * gate_gain
    hidden = (up_proj * jax.nn.silu(gate_proj)).astype(jnp.bfloat16)
    mixed_sum = lax.psum_scatter(
        jnp.dot(hidden, w_down, preferred_element_type=jnp.float32).astype(jnp.bfloat16),
        "dp",
        scatter_dimension=0,
        tiled=True,
    ).astype(jnp.float32)
    mlp_rows = normalize(mixed_sum)
    residual_mid = mid_rows.astype(jnp.float32)
    result_rows = normalize(residual_mid + alpha_mlp * (mlp_rows - residual_mid)).astype(
        jnp.bfloat16
    )
    request_ends = jnp.cumsum(tally) - 1
    same_request = segments[:, None] == request_numbers[None, :]
    row_end = jnp.sum(jnp.where(same_request, request_ends[None, :], 0), axis=1)
    is_last = positions == row_end
    member = same_request.astype(jnp.float32)
    chosen = member * is_last[:, None].astype(jnp.float32)
    result_f32 = result_rows.astype(jnp.float32)
    row_sums = jnp.dot(member.T, result_f32, precision=lax.Precision.HIGHEST)
    last_rows = jnp.dot(chosen.T, result_f32, precision=lax.Precision.HIGHEST)
    counts = jnp.sum(member, axis=0)
    row_sums, last_rows, counts = (
        lax.psum(row_sums.astype(jnp.bfloat16), "tensor").astype(jnp.float32),
        lax.psum(last_rows.astype(jnp.bfloat16), "tensor").astype(jnp.float32),
        lax.psum(counts.astype(jnp.bfloat16), "tensor").astype(jnp.float32),
    )
    request_mean = row_sums / counts[:, None]
    group_norm = jnp.sqrt(jnp.mean(request_mean * request_mean, axis=1))
    slot_count = lax.axis_size("dp") * REQS
    every_last, every_norm = (
        lax.all_gather(last_rows, "dp", axis=0, tiled=True),
        lax.all_gather(group_norm, "dp", axis=0, tiled=True),
    )
    logits = jnp.dot(
        every_last.astype(jnp.bfloat16), w_vocab, preferred_element_type=jnp.float32
    ) * logit_gain.astype(jnp.float32)
    every_max = lax.pmax(jnp.max(logits, axis=1), ("dp", "tensor"))
    placement = (pack_of_group[:, None] == jnp.arange(slot_count, dtype=jnp.int32)[None, :]).astype(
        jnp.float32
    )
    request_norm = jnp.dot(every_norm, placement, precision=lax.Precision.HIGHEST)
    max_logit = jnp.dot(every_max, placement, precision=lax.Precision.HIGHEST)
    return (result_rows[None], request_norm, max_logit)


def solution(mesh):
    return jax.shard_map(
        local,
        mesh=mesh,
        in_specs=(
            P("dp", "tensor", None),
            P("dp", "tensor"),
            P(),
            P(),
            P(),
            P(),
            P(),
            P(None, "dp"),
            P(None, "dp"),
            P("dp"),
            P("dp"),
            P("dp", None),
            P(),
            P(None, ("dp", "tensor")),
            P(("dp", "tensor")),
        ),
        out_specs=(P("dp", "tensor", None), P(), P()),
        check_vma=False,
    )
```

profile of v0, /device:TPU:1, one launch (start us, length us, event | category | flops | bytes accessed | tf_op | source)
XLA Modules:
  0.0 689.7 jit_solution(16697699601182889394)
XLA Ops:
  8.5 3.4 fusion.186
  14.2 46.0 %all-gather = s32[1,4096]{1,0:T(1,128)S(1)} all-gather(s32[1,128]{1,0:T(1,128)S(1)} %copy-done.26), channel_id=2, replica_groups=mesh['dp'=8,'tensor'=32] {'tensor'}, dimensions={1}, use_global_device_ids=true | all-gather | bytes 16896 | tf_op jit(solution)/shard_map/all_gather | solution.py:65
  61.7 19.2 %all-gather.8.cloned.1.call-done = bf16[4096,640]{1,0:T(8,128)(2,1)} async-done(((bf16[128,640]{1,0:T(8,128)(2,1)}), bf16[4096,640]{1,0:T(8,128)(2,1)}) %all-gather.8.cloned.1.call-update) | async-done | bytes 5242896 | tf_op jit(solution)/shard_map/all_gather | solution.py:64
  80.8 4.5 fusion.191
  85.3 2.2 copy.88
  87.5 58.2 %all-gather.6.cloned.1.call-done = bf16[4096,640]{1,0:T(8,128)(2,1)} async-done(((bf16[128,640]{1,0:T(8,128)(2,1)}), bf16[4096,640]{1,0:T(8,128)(2,1)}) %all-gather.6.cloned.1.call-update) | async-done | bytes 5242896 | tf_op jit(solution)/shard_map/all_gather | solution.py:63
  145.7 4.9 fusion.192
  150.6 2.2 copy.77
  152.8 2.2 copy.91
  157.1 2.2 copy.87
  159.3 2.2 copy.85
  161.5 2.2 copy.83
  163.7 2.2 copy.81
  168.1 2.2 copy.92
  174.6 2.2 copy.84
  176.8 2.2 copy.82
  206.1 81.0 %all-gather.10.cloned.1.call-done = bf16[1024,1280]{1,0:T(8,128)(2,1)} async-done(((bf16[128,1280]{1,0:T(8,128)(2,1)}), bf16[1024,1280]{1,0:T(8,128)(2,1)}) %all-gather.10.cloned.1.call-update) | async-done | bytes 2621456 | tf_op jit(solution)/shard_map/all_gather | solution.py:109
  287.2 5.9 fusion.194
  293.1 8.4 %convolution_convert_fusion = bf16[1024,1280]{1,0:T(8,128)(2,1)} fusion(bf16[640,1280]{1,0:T(8,128)(2,1)S(1)} %copy-done, f32[1024,640]{1,0:T(8,128)} %fusion.194, bf16[1024,1280]{1,0:T(8,128)(2,1)} %all-gather.10.cloned.1.call-done, bf16[1280,640]{1,0:T(8,128)(2,1)S(1)} %copy-done.27, f32[640]{0:T(1024)S(1)} %copy-done.28, f32[640]{0:T(1024)S(1)} %copy-done.29), kind=kOutput, calls=%fused_computation | convolution fusion | flops 3361996800 | bytes 11146240 | tf_op jit(solution)/shard_map/dot_general | solution.py:114
  304.0 94.9 %reduce-scatter.2.cloned.1.call-done = bf16[128,1280]{1,0:T(8,128)(2,1)} async-done(((bf16[1024,1280]{1,0:T(8,128)(2,1)}), bf16[128,1280]{1,0:T(8,128)(2,1)}) %reduce-scatter.2.cloned.1.call-update) | async-done | bytes 327696 | tf_op jit(solution)/shard_map/reduce_scatter | solution.py:113
  403.2 130.5 %all-reduce.1 = (bf16[4,1280]{1,0:T(4,128)(2,1)S(1)}, bf16[4]{0:T(256)(128)(2,1)S(1)}, bf16[4,1280]{1,0:T(4,128)(2,1)S(1)}) all-reduce(bf16[4,1280]{1,0:T(4,128)(2,1)S(1)} %convolution_convert_fusion.2, bf16[4]{0:T(256)(128)(2,1)S(1)} %convert_reduce_fusion.1, ...), channel_id=1, replica_groups=mesh['dp'=8,'tensor'=32] {'tensor'}, use_global_device_ids=true, to_apply=%region_24.25 | all-reduce | flops 10244 | bytes 40976 | tf_op jit(solution)/shard_map/psum | solution.py:135
  533.7 37.8 %all-gather.1 = bf16[8,4,1280]{2,1,0:T(4,128)(2,1)S(1)} all-gather(bf16[1,4,1280]{2,1,0:T(4,128)(2,1)S(1)} %bitcast.282), channel_id=1, replica_groups=mesh['dp'=8,'tensor'=32] {'dp'}, dimensions={0}, use_global_device_ids=true | all-gather | bytes 92160 | tf_op jit(solution)/shard_map/all_gather | solution.py:143
  572.1 23.2 %all-reduce = f32[32]{0:T(128)S(1)} all-reduce(f32[32]{0:T(128)S(1)} %sqrt_dynamic-update-slice_fusion), channel_id=1, replica_groups=mesh['dp'=8,'tensor'=32] {'dp'}, use_global_device_ids=true, to_apply=%add | all-reduce | flops 32 | bytes 256
  595.3 86.5 %pmax.7 = f32[32]{0:T(128)S(1)} all-reduce(f32[32]{0:T(128)S(1)} %fusion.133), channel_id=1, replica_groups=mesh['dp'=8,'tensor'=32] {'dp','tensor'}, use_global_device_ids=true, to_apply=%region_33.34 | all-reduce | flops 32 | bytes 256 | tf_op jit(solution)/shard_map/pmax | solution.py:149
  (156 shorter events, 48.4 us)
Async XLA Ops:
  7.2 285.9 %copy-start = (bf16[640,1280]{1,0:T(8,128)(2,1)S(1)}, bf16[640,1280]{1,0:T(8,128)(2,1)}, u32[]{:S(2)}) copy-start(bf16[640,1280]{1,0:T(8,128)(2,1)} %param.26) | copy-start | bytes 4915204
  7.2 73.7 %all-gather.8.cloned.1.call-start = ((), (), s32[]{:S(2)}) async-start(), calls=%async_computation.2 | async-start | bytes 5406720 | tf_op jit(solution)/shard_map/all_gather | solution.py:64
  11.9 1.2 copy-start.25
  12.6 1.6 copy-start.26
  12.6 133.1 %all-gather.6.cloned.1.call-start = ((), (), s32[]{:S(2)}) async-start(), calls=%async_computation.1 | async-start | bytes 5406720 | tf_op jit(solution)/shard_map/all_gather | solution.py:63
  13.9 273.3 %all-gather.10.cloned.1.call-start = ((), (), s32[]{:S(2)}) async-start(), calls=%async_computation.3 | async-start | bytes 2949120 | tf_op jit(solution)/shard_map/all_gather | solution.py:109
  180.1 2.9 copy-start.10
  181.2 1.8 copy-start.21
  190.2 1.8 copy-start.18
  193.8 1.6 copy-start.15
  197.3 1.6 copy-start.14
  199.7 1.7 copy-start.13
  202.5 1.4 copy-start.11
  202.5 2.0 copy-start.23
  203.3 1.2 copy-start.1
  205.8 87.3 %copy-start.27 = (bf16[1280,640]{1,0:T(8,128)(2,1)S(1)}, bf16[1280,640]{1,0:T(8,128)(2,1)}, u32[]{:S(2)}) copy-start(bf16[1280,640]{1,0:T(8,128)(2,1)} %param.23) | copy-start | bytes 4915204
  205.8 87.2 %copy-start.28 = (f32[640]{0:T(1024)S(1)}, f32[640]{0:T(1024)}, u32[]{:S(2)}) copy-start(f32[640]{0:T(1024)} %param.25) | copy-start | bytes 7684
  205.8 87.2 %copy-start.29 = (f32[640]{0:T(1024)S(1)}, f32[640]{0:T(1024)}, u32[]{:S(2)}) copy-start(f32[640]{0:T(1024)} %param.24) | copy-start | bytes 7684
  205.9 193.1 %reduce-scatter.2.cloned.1.call-start = ((), (), s32[]{:S(2)}) async-start(), calls=%async_computation.4 | async-start | bytes 2949120 | tf_op jit(solution)/shard_map/reduce_scatter | solution.py:113
  301.5 98.5 %copy-start.2 = (bf16[128,1280]{1,0:T(8,128)(2,1)S(1)}, bf16[128,1280]{1,0:T(8,128)(2,1)}, u32[]{:S(2)}) copy-start(bf16[128,1280]{1,0:T(8,128)(2,1)} %multiply_convert_fusion.2) | copy-start | bytes 983044
  301.5 98.5 %copy-start.24 = (f32[1280]{0:T(1024)S(1)}, f32[1280]{0:T(1024)}, u32[]{:S(2)}) copy-start(f32[1280]{0:T(1024)} %param.27) | copy-start | bytes 15364
  301.5 270.3 %copy-start.22 = (bf16[1280,125]{1,0:T(8,128)(2,1)S(1)}, bf16[1280,125]{1,0:T(8,128)(2,1)}, u32[]{:S(2)}) copy-start(bf16[1280,125]{1,0:T(8,128)(2,1)} %param.28) | copy-start | bytes 960004
  301.5 380.2 %copy-start.31 = (s32[32]{0:T(128)S(1)}, s32[32]{0:T(128)}, u32[]{:S(2)}) copy-start(s32[32]{0:T(128)} %param.17) | copy-start | bytes 388
  402.8 280.4 %copy-start.3 = (bf16[128,1280]{1,0:T(8,128)(2,1)}, bf16[128,1280]{1,0:T(8,128)(2,1)S(1)}, u32[]{:S(2)}) copy-start(bf16[128,1280]{1,0:T(8,128)(2,1)S(1)} %multiply_convert_fusion.1) | copy-start | bytes 983044
  (13 other events, 13.6 us)
Sparse Core Ops, SparseCore 0:
  12.7 68.0 all-gather.7
  82.7 62.9 all-gather.5
  205.9 81.1 all-gather.9
  301.7 97.1 reduce-scatter.1
where the time goes:
time: 691 us; the launch traced here: 690 us
  blocking collectives  324 us (47%)
  waiting for transfers between devices  253 us (37%)
  local copies, waits for them, and re-layouts  47.8 us (7%)
  matrix products  33 us (5%)
  other arithmetic  16.1 us (2%)
  between operations  15 us (2%)
    psum x1, blocking collectives, local(): lax.psum(row_sums.astype(jnp.bfloat16), 'tensor').astype(jnp.float32)  131 us
    reduce_scatter x1, waiting for transfers between devices, local(): lax.psum_scatter(jnp.dot(hidden, w_down, preferred_element_type=jnp.float...  94.9 us
    pmax x1, blocking collectives, local(): every_max = lax.pmax(jnp.max(logits, axis=1), ('dp', 'tensor'))  86.5 us
    all_gather x1, waiting for transfers between devices, local(): received = lax.all_gather(mid_rows, 'dp', axis=0, tiled=True)  81 us
    all_gather x1, waiting for transfers between devices, local(): key_all = lax.all_gather(key_rows, 'tensor', axis=0, tiled=True)  58.2 us
    all_gather x1, blocking collectives, local(): seg_all = lax.all_gather(segments, 'tensor', axis=0, tiled=True)  46 us
    all_gather x1, blocking collectives, local(): lax.all_gather(last_rows, 'dp', axis=0, tiled=True)  37.8 us
    unnamed x1, blocking collectives  23.2 us
  transfers between devices with their start and end apart: 4, of which 4 were waited for; matrix products, arithmetic and copies ran while one was open for 2% of the time, Pallas kernels for 0%

commit v1 on v0

--- a/solution.py
+++ b/solution.py
@@ -60,9 +60,16 @@
         jnp.zeros((HEADS, row_count), jnp.float32),
         jnp.zeros((HEADS, row_count, HD), jnp.float32),
     )
-    key_all = lax.all_gather(key_rows, "tensor", axis=0, tiled=True)
-    value_all = lax.all_gather(value_rows, "tensor", axis=0, tiled=True)
-    seg_all = lax.all_gather(segments, "tensor", axis=0, tiled=True)
+    seg_block = jnp.zeros((8, 2 * head_width), jnp.bfloat16).at[0, :row_count].set(
+        segments.astype(jnp.bfloat16)
+    )
+    packed = jnp.concatenate(
+        [jnp.concatenate([key_rows, value_rows], axis=1), seg_block], axis=0
+    )
+    gathered = lax.all_gather(packed, "tensor", axis=0, tiled=False)
+    key_all = gathered[:, :row_count, :head_width].reshape(-1, head_width)
+    value_all = gathered[:, :row_count, head_width:].reshape(-1, head_width)
+    seg_all = gathered[:, row_count, :row_count].reshape(-1).astype(jnp.int32)
     tally = jnp.sum((seg_all[:, None] == request_numbers[None, :]).astype(jnp.int32), axis=0)
     total_keys = key_all.shape[0]
     step_size = math.gcd(total_keys, 512)
@@ -130,19 +137,19 @@
     result_f32 = result_rows.astype(jnp.float32)
     row_sums = jnp.dot(member.T, result_f32, precision=lax.Precision.HIGHEST)
     last_rows = jnp.dot(chosen.T, result_f32, precision=lax.Precision.HIGHEST)
-    counts = jnp.sum(member, axis=0)
-    row_sums, last_rows, counts = (
-        lax.psum(row_sums.astype(jnp.bfloat16), "tensor").astype(jnp.float32),
-        lax.psum(last_rows.astype(jnp.bfloat16), "tensor").astype(jnp.float32),
-        lax.psum(counts.astype(jnp.bfloat16), "tensor").astype(jnp.float32),
-    )
+    partial = jnp.concatenate([row_sums, last_rows], axis=0)
+    summed = jnp.sum(lax.all_gather(partial, "tensor", axis=0, tiled=False), axis=0)
+    row_sums, last_rows = summed[:REQS], summed[REQS:]
+    counts = tally.astype(jnp.float32)
     request_mean = row_sums / counts[:, None]
     group_norm = jnp.sqrt(jnp.mean(request_mean * request_mean, axis=1))
     slot_count = lax.axis_size("dp") * REQS
-    every_last, every_norm = (
-        lax.all_gather(last_rows, "dp", axis=0, tiled=True),
-        lax.all_gather(group_norm, "dp", axis=0, tiled=True),
+    norm_row = jnp.zeros((1, last_rows.shape[1]), jnp.float32).at[0, :REQS].set(group_norm)
+    pack_stats = lax.all_gather(
+        jnp.concatenate([last_rows, norm_row], axis=0), "dp", axis=0, tiled=False
     )
+    every_last = pack_stats[:, :REQS].reshape(slot_count, -1)
+    every_norm = pack_stats[:, REQS, :REQS].reshape(slot_count)
     logits = jnp.dot(
         every_last.astype(jnp.bfloat16), w_vocab, preferred_element_type=jnp.float32
     ) * logit_gain.astype(jnp.float32)

time: 691 us -> 607 us (0.88); the launches traced: 690 us -> 599 us
  blocking collectives: 324 us -> 120 us
  waiting for transfers between devices: 253 us -> 307 us
  local copies, waits for them, and re-layouts: 47.8 us -> 77.6 us
  matrix products: 33 us -> 48.5 us
  other arithmetic: 16.1 us -> 30 us
    psum x1 -> x0, blocking collectives: 131 us -> none  [local(): lax.psum(row_sums.astype(jnp.bfloat16), 'tensor').astype(jnp.float32)]
    all_gather x2, waiting for transfers between devices: 77.4 us -> 129 us  [the longest x1 72.6 us: local(): gathered = lax.all_gather(packed, 'tensor', axis=0, tiled=False)]
    all_gather x2 -> x1, blocking collectives: 83.8 us -> 38.8 us  [local(): lax.all_gather(jnp.concatenate([last_rows, norm_row], axis=0), 'dp', axis...]
    reshape x0 -> x16, local copies, waits for them, and re-layouts: none -> 34.5 us  [the longest x8 18.2 us: local(): key_heads = key_part.reshape(key_count, HEADS, HD)]
    unnamed x1 -> x0, blocking collectives: 23.2 us -> none
    dot_general x8, matrix products: 6.49 us -> 15.1 us  [local(): jnp.einsum('qhd,khd->hqk', queries, key_heads, preferred_element_type=jnp...]
    dot_general x8, matrix products: 6.13 us -> 13.1 us  [local(): jnp.einsum('hqk,khd->hqd', weights.astype(jnp.bfloat16), value_heads, pre...]
    slice x9 -> x8, local copies, waits for them, and re-layouts: 22.4 us -> 17 us  [local(): key_part = key_all[begin:begin + step_size]]
  transfers between devices with their start and end apart: 4 -> 4, of which waited for: 4 -> 4; matrix products, arithmetic and copies ran while one was open for 2% -> 1% of each run, Pallas kernels for 0% -> 0%
where the time goes in v1:
time: 607 us; the launch traced here: 599 us
  waiting for transfers between devices  307 us (51%)
  blocking collectives  120 us (20%)
  local copies, waits for them, and re-layouts  77.6 us (13%)
  matrix products  48.5 us (8%)
  other arithmetic  30 us (5%)
  between operations  15 us (2%)
    reduce_scatter x1, waiting for transfers between devices, local(): lax.psum_scatter(jnp.dot(hidden, w_down, preferred_element_type=jnp.float...  96.4 us
    pmax x1, blocking collectives, local(): every_max = lax.pmax(jnp.max(logits, axis=1), ('dp', 'tensor'))  81.2 us
    all_gather x1, waiting for transfers between devices, local(): received = lax.all_gather(mid_rows, 'dp', axis=0, tiled=True)  81.2 us
    all_gather x1, waiting for transfers between devices, local(): gathered = lax.all_gather(packed, 'tensor', axis=0, tiled=False)  72.6 us
    all_gather x1, waiting for transfers between devices, local(): lax.all_gather(partial, 'tensor', axis=0, tiled=False)  56.6 us
    all_gather x1, blocking collectives, local(): lax.all_gather(jnp.concatenate([last_rows, norm_row], axis=0), 'dp', axis...  38.8 us
    slice x9, local copies, waits for them, and re-layouts, local(): value_part = value_all[begin:begin + step_size]  22.8 us
    reshape x8, local copies, waits for them, and re-layouts, local(): key_heads = key_part.reshape(key_count, HEADS, HD)  18.2 us
  transfers between devices with their start and end apart: 4, of which 4 were waited for; matrix products, arithmetic and copies ran while one was open for 1% of the time, Pallas kernels for 0%

profile of v1, /device:TPU:1, one launch (start us, length us, event | category | flops | bytes accessed | tf_op | source)
XLA Modules:
  0.0 598.5 jit_solution(7034358998079594699)
XLA Ops:
  8.5 3.4 fusion.191
  18.6 72.6 %all-gather.10.cloned.1.call-done = bf16[4352,1280]{1,0:T(8,128)(2,1)} async-done(((bf16[136,1280]{1,0:T(8,128)(2,1)}), bf16[4352,1280]{1,0:T(8,128)(2,1)}) %all-gather.10.cloned.1.call-update) | async-done | bytes 11141136 | tf_op jit(solution)/shard_map/all_gather | solution.py:69
  91.2 7.8 %fusion.196 = (bf16[4,128,640]{2,1,0:T(8,128)(2,1)S(1)}, bf16[4,128,640]{2,1,0:T(8,128)(2,1)}, bf16[4,128,640]{2,1,0:T(8,128)(2,1)}, bf16[4,128,640]{2,1,0:T(8,1...) fusion(bf16[32,136,1280]{2,1,0:T(8,128)(2,1)} %bitcast.275), kind=kLoop, calls=%fused_computation.238 | loop fusion | bytes 20971520 | tf_op jit(solution)/shard_map/slice | solution.py:78
  102.0 2.3 reshape.991
  106.4 2.3 reshape.990
  110.8 2.3 reshape.988
  115.2 2.3 reshape.986
  119.6 2.3 reshape.984
  124.0 2.3 reshape.982
  141.6 2.4 reshape.989
  169.4 2.3 reshape.985
  178.2 2.3 reshape.981
  180.4 3.5 fusion.100
  183.9 3.7 fusion.4
  194.9 2.3 reshape.977
  198.3 2.8 fusion.103
  201.2 3.1 fusion.8
  212.4 81.2 %all-gather.8.cloned.1.call-done = bf16[1024,1280]{1,0:T(8,128)(2,1)} async-done(((bf16[128,1280]{1,0:T(8,128)(2,1)}), bf16[1024,1280]{1,0:T(8,128)(2,1)}) %all-gather.8.cloned.1.call-update) | async-done | bytes 2621456 | tf_op jit(solution)/shard_map/all_gather | solution.py:116
  293.6 5.9 fusion.200
  299.5 8.4 %convolution_convert_fusion = bf16[1024,1280]{1,0:T(8,128)(2,1)} fusion(bf16[640,1280]{1,0:T(8,128)(2,1)S(1)} %copy-done, f32[1024,640]{1,0:T(8,128)} %fusion.200, bf16[1024,1280]{1,0:T(8,128)(2,1)} %all-gather.8.cloned.1.call-done, bf16[1280,640]{1,0:T(8,128)(2,1)S(1)} %copy-done.46, f32[640]{0:T(1024)S(1)} %copy-done.47, f32[640]{0:T(1024)S(1)} %copy-done.48), kind=kOutput, calls=%fused_computation | convolution fusion | flops 3361996800 | bytes 11146240 | tf_op jit(solution)/shard_map/dot_general | solution.py:121
  308.7 96.4 %reduce-scatter.2.cloned.1.call-done = bf16[128,1280]{1,0:T(8,128)(2,1)} async-done(((bf16[1024,1280]{1,0:T(8,128)(2,1)}), bf16[128,1280]{1,0:T(8,128)(2,1)}) %reduce-scatter.2.cloned.1.call-update) | async-done | bytes 327696 | tf_op jit(solution)/shard_map/reduce_scatter | solution.py:120
  410.7 56.6 %all-gather.12.cloned.1.call-done = f32[256,1280]{1,0:T(8,128)} async-done(((f32[8,1280]{1,0:T(8,128)}), f32[256,1280]{1,0:T(8,128)}) %all-gather.12.cloned.1.call-update) | async-done | bytes 1310736 | tf_op jit(solution)/shard_map/all_gather | solution.py:141
  469.6 38.8 %all-gather.3 = f32[8,5,1280]{2,1,0:T(8,128)S(1)} all-gather(f32[1,5,1280]{2,1,0:T(8,128)S(1)} %fusion.148), channel_id=4, replica_groups=mesh['dp'=8,'tensor'=32] {'dp'}, dimensions={0}, use_global_device_ids=true | all-gather | bytes 230400 | tf_op jit(solution)/shard_map/all_gather | solution.py:148
  508.9 81.2 %pmax.7 = f32[32]{0:T(128)S(1)} all-reduce(f32[32]{0:T(128)S(1)} %fusion.133), channel_id=1, replica_groups=mesh['dp'=8,'tensor'=32] {'dp','tensor'}, use_global_device_ids=true, to_apply=%region_31.32 | all-reduce | flops 32 | bytes 256 | tf_op jit(solution)/shard_map/pmax | solution.py:156
  (219 shorter events, 95.1 us)
Async XLA Ops:
  7.2 292.4 %copy-start = (bf16[640,1280]{1,0:T(8,128)(2,1)S(1)}, bf16[640,1280]{1,0:T(8,128)(2,1)}, u32[]{:S(2)}) copy-start(bf16[640,1280]{1,0:T(8,128)(2,1)} %param.30) | copy-start | bytes 4915204
  7.2 84.0 %all-gather.10.cloned.1.call-start = ((), (), s32[]{:S(2)}) async-start(), calls=%async_computation.3 | async-start | bytes 11489280 | tf_op jit(solution)/shard_map/all_gather | solution.py:69
  8.5 3.4 copy-start.42
  8.5 3.5 copy-start.44
  13.5 280.1 %all-gather.8.cloned.1.call-start = ((), (), s32[]{:S(2)}) async-start(), calls=%async_computation.1 | async-start | bytes 2949120 | tf_op jit(solution)/shard_map/all_gather | solution.py:116
  147.8 13.7 %copy-start.23 = (f32[10,128]{1,0:T(8,128)}, f32[10,128]{1,0:T(8,128)S(1)}, u32[]{:S(2)}) copy-start(f32[10,128]{1,0:T(8,128)S(1)} %get-tuple-element.84) | copy-start | bytes 15364
  150.3 11.2 %copy-start.25 = (f32[10,128]{1,0:T(8,128)}, f32[10,128]{1,0:T(8,128)S(1)}, u32[]{:S(2)}) copy-start(f32[10,128]{1,0:T(8,128)S(1)} %get-tuple-element.86) | copy-start | bytes 15364
  158.8 3.4 copy-start.17
  180.4 3.5 copy-start.4
  183.9 3.7 copy-start.5
  183.9 3.7 copy-start.21
  193.5 4.8 copy-start.33
  201.1 3.2 copy-start.3
  212.3 87.2 %copy-start.46 = (bf16[1280,640]{1,0:T(8,128)(2,1)S(1)}, bf16[1280,640]{1,0:T(8,128)(2,1)}, u32[]{:S(2)}) copy-start(bf16[1280,640]{1,0:T(8,128)(2,1)} %param.27) | copy-start | bytes 4915204
  212.3 87.2 %copy-start.47 = (f32[640]{0:T(1024)S(1)}, f32[640]{0:T(1024)}, u32[]{:S(2)}) copy-start(f32[640]{0:T(1024)} %param.29) | copy-start | bytes 7684
  212.3 87.2 %copy-start.48 = (f32[640]{0:T(1024)S(1)}, f32[640]{0:T(1024)}, u32[]{:S(2)}) copy-start(f32[640]{0:T(1024)} %param.28) | copy-start | bytes 7684
  212.4 192.8 %reduce-scatter.2.cloned.1.call-start = ((), (), s32[]{:S(2)}) async-start(), calls=%async_computation.2 | async-start | bytes 2949120 | tf_op jit(solution)/shard_map/reduce_scatter | solution.py:120
  308.0 98.3 %copy-start.7 = (bf16[128,1280]{1,0:T(8,128)(2,1)S(1)}, bf16[128,1280]{1,0:T(8,128)(2,1)}, u32[]{:S(2)}) copy-start(bf16[128,1280]{1,0:T(8,128)(2,1)} %multiply_convert_fusion.2) | copy-start | bytes 983044
  308.0 98.3 %copy-start.36 = (f32[1280]{0:T(1024)S(1)}, f32[1280]{0:T(1024)}, u32[]{:S(2)}) copy-start(f32[1280]{0:T(1024)} %param.31) | copy-start | bytes 15364
  308.0 102.1 %copy-start.49 = (bf16[125]{0:T(256)(128)(2,1)S(1)}, bf16[125]{0:T(256)(128)(2,1)}, u32[]{:S(2)}) copy-start(bf16[125]{0:T(256)(128)(2,1)} %param.33) | copy-start | bytes 754
  308.0 200.5 %copy-start.22 = (bf16[1280,125]{1,0:T(8,128)(2,1)S(1)}, bf16[1280,125]{1,0:T(8,128)(2,1)}, u32[]{:S(2)}) copy-start(bf16[1280,125]{1,0:T(8,128)(2,1)} %param.32) | copy-start | bytes 960004
  308.0 159.3 %all-gather.12.cloned.1.call-start = ((), (), s32[]{:S(2)}) async-start(), calls=%async_computation.4 | async-start | bytes 1351680 | tf_op jit(solution)/shard_map/all_gather | solution.py:141
  406.3 183.9 %copy-start.50 = (s32[32]{0:T(128)S(1)}, s32[32]{0:T(128)}, u32[]{:S(2)}) copy-start(s32[32]{0:T(128)} %param.21) | copy-start | bytes 388
  409.0 182.6 %copy-start.8 = (bf16[128,1280]{1,0:T(8,128)(2,1)}, bf16[128,1280]{1,0:T(8,128)(2,1)S(1)}, u32[]{:S(2)}) copy-start(bf16[128,1280]{1,0:T(8,128)(2,1)S(1)} %multiply_convert_fusion.1) | copy-start | bytes 983044
  (35 other events, 66.0 us)
Sparse Core Ops, SparseCore 0:
  13.6 77.5 all-gather.9
  212.4 81.1 all-gather.7
  308.1 96.9 reduce-scatter.1
  410.2 57.0 all-gather.11

commit v2 on v1

--- a/solution.py
+++ b/solution.py
@@ -54,12 +54,6 @@
     )
     value_rows = projected[:, 2 * head_width :].astype(jnp.bfloat16)
     score_scale = 1.0 / math.sqrt(HD)
-    offset = jnp.int32(0)
-    state_now = (
-        jnp.full((HEADS, row_count), NEGATIVE, jnp.float32),
-        jnp.zeros((HEADS, row_count), jnp.float32),
-        jnp.zeros((HEADS, row_count, HD), jnp.float32),
-    )
     seg_block = jnp.zeros((8, 2 * head_width), jnp.bfloat16).at[0, :row_count].set(
         segments.astype(jnp.bfloat16)
     )
@@ -72,38 +66,23 @@
     seg_all = gathered[:, row_count, :row_count].reshape(-1).astype(jnp.int32)
     tally = jnp.sum((seg_all[:, None] == request_numbers[None, :]).astype(jnp.int32), axis=0)
     total_keys = key_all.shape[0]
-    step_size = math.gcd(total_keys, 512)
-    for begin in range(0, total_keys, step_size):
-        key_part = key_all[begin : begin + step_size]
-        value_part = value_all[begin : begin + step_size]
-        seg_part = seg_all[begin : begin + step_size]
-        key_pos = offset + begin + jnp.arange(step_size, dtype=jnp.int32)
-        update_running_max, update_weight_sum, update_weighted = state_now
-        key_count = key_part.shape[0]
-        key_heads = key_part.reshape(key_count, HEADS, HD)
-        value_heads = value_part.reshape(key_count, HEADS, HD)
-        scores = (
-            jnp.einsum("qhd,khd->hqk", queries, key_heads, preferred_element_type=jnp.float32)
-            * score_scale
-        )
-        allowed = (seg_part[None, :] == segments[:, None]) & (
-            key_pos[None, :] <= positions[:, None]
-        )
-        new_max = jnp.maximum(
-            update_running_max, jnp.max(jnp.where(allowed[None], scores, NEGATIVE), axis=2)
-        )
-        weights = jnp.where(allowed[None], jnp.exp(scores - new_max[:, :, None]), 0.0)
-        factor = jnp.exp(update_running_max - new_max)
-        update_weight_sum = update_weight_sum * factor + jnp.sum(weights, axis=2)
-        update_weighted = update_weighted * factor[:, :, None] + jnp.einsum(
-            "hqk,khd->hqd",
-            weights.astype(jnp.bfloat16),
-            value_heads,
-            preferred_element_type=jnp.float32,
-        )
-        state_now = (new_max, update_weight_sum, update_weighted)
-    folded, tally = (state_now, tally)
-    running_max, weight_sum, weighted = folded
+    key_pos = jnp.arange(total_keys, dtype=jnp.int32)
+    key_heads = key_all.reshape(total_keys, HEADS, HD)
+    value_heads = value_all.reshape(total_keys, HEADS, HD)
+    scores = (
+        jnp.einsum("qhd,khd->hqk", queries, key_heads, preferred_element_type=jnp.float32)
+        * score_scale
+    )
+    allowed = (seg_all[None, :] == segments[:, None]) & (key_pos[None, :] <= positions[:, None])
+    row_max = jnp.max(jnp.where(allowed[None], scores, NEGATIVE), axis=2)
+    weights = jnp.where(allowed[None], jnp.exp(scores - row_max[:, :, None]), 0.0)
+    weight_sum = jnp.sum(weights, axis=2)
+    weighted = jnp.einsum(
+        "hqk,khd->hqd",
+        weights.astype(jnp.bfloat16),
+        value_heads,
+        preferred_element_type=jnp.float32,
+    )
     attended = (
         (weighted / weight_sum[:, :, None])
         .transpose(1, 0, 2)

time: 607 us -> 555 us (0.914); the launches traced: 599 us -> 554 us
  local copies, waits for them, and re-layouts: 77.6 us -> 45.8 us
  other arithmetic: 30 us -> 12.6 us
    reshape x16 -> x0, local copies, waits for them, and re-layouts: 34.5 us -> none  [the longest x8 18.2 us: local(): key_heads = key_part.reshape(key_count, HEADS, HD)]
    sub x0 -> x1, matrix products: none -> 19.1 us  [local(): scores - row_max[:, :, None]]
    another operation x0 -> x2, local copies, waits for them, and re-layouts: none -> 17.6 us  [the longest x1 8.82 us: local(): value_heads = value_all.reshape(total_keys, HEADS, HD)]
    dot_general x8 -> x0, matrix products: 15.1 us -> none  [local(): jnp.einsum('qhd,khd->hqk', queries, key_heads, preferred_element_type=jnp...]
    slice x18 -> x3, local copies, waits for them, and re-layouts: 39.8 us -> 26.8 us  [the longest x2 18.2 us: local(): key_all = gathered[:, :row_count, :head_width].reshape(-1, head_width)]
    reduce_sum x4 -> x0, other arithmetic: 10.6 us -> none  [local(): update_weight_sum = update_weight_sum * factor + jnp.sum(weights, axis=2)]
    dot_general x8 -> x1, matrix products: 13.1 us -> 9.29 us  [local(): jnp.einsum('hqk,khd->hqd', weights.astype(jnp.bfloat16), value_heads, pre...]
  transfers between devices with their start and end apart: 4 -> 4, of which waited for: 4 -> 4; matrix products, arithmetic and copies ran while one was open for 1% -> 0% of each run, Pallas kernels for 0% -> 0%
where the time goes in v2:
time: 555 us; the launch traced here: 554 us
  waiting for transfers between devices  312 us (56%)
  blocking collectives  120 us (22%)
  matrix products  49.3 us (9%)
  local copies, waits for them, and re-layouts  45.8 us (8%)
  between operations  14.1 us (3%)
  other arithmetic  12.6 us (2%)
    reduce_scatter x1, waiting for transfers between devices, local(): lax.psum_scatter(jnp.dot(hidden, w_down, preferred_element_type=jnp.float...  96.8 us
    pmax x1, blocking collectives, local(): every_max = lax.pmax(jnp.max(logits, axis=1), ('dp', 'tensor'))  81.3 us
    all_gather x1, waiting for transfers between devices, local(): received = lax.all_gather(mid_rows, 'dp', axis=0, tiled=True)  81 us
    all_gather x1, waiting for transfers between devices, local(): gathered = lax.all_gather(packed, 'tensor', axis=0, tiled=False)  77.4 us
    all_gather x1, waiting for transfers between devices, local(): lax.all_gather(partial, 'tensor', axis=0, tiled=False)  56.6 us
    all_gather x1, blocking collectives, local(): lax.all_gather(jnp.concatenate([last_rows, norm_row], axis=0), 'dp', axis...  38.8 us
    sub x1, matrix products, local(): scores - row_max[:, :, None]  19.1 us
    slice x2, local copies, waits for them, and re-layouts, local(): key_all = gathered[:, :row_count, :head_width].reshape(-1, head_width)  18.2 us
  transfers between devices with their start and end apart: 4, of which 4 were waited for; matrix products, arithmetic and copies ran while one was open for 0% of the time, Pallas kernels for 0%

profile of v2, /device:TPU:1, one launch (start us, length us, event | category | flops | bytes accessed | tf_op | source)
XLA Modules:
  0.0 554.1 jit_solution(5933065221642050692)
XLA Ops:
  7.2 1.2 fusion.27
  8.5 3.4 fusion.48
  12.7 0.8 fusion.29
  13.8 77.4 %all-gather.10.cloned.1.call-done = bf16[4352,1280]{1,0:T(8,128)(2,1)} async-done(((bf16[136,1280]{1,0:T(8,128)(2,1)}), bf16[4352,1280]{1,0:T(8,128)(2,1)}) %all-gather.10.cloned.1.call-update) | async-done | bytes 11141136 | tf_op jit(solution)/shard_map/all_gather | solution.py:63
  91.2 0.9 slice_convert_fusion.2
  92.1 9.7 %fusion.50 = (bf16[32,128,640]{2,1,0:T(8,128)(2,1)}, bf16[32,128,640]{2,1,0:T(8,128)(2,1)}) fusion(bf16[32,136,1280]{2,1,0:T(8,128)(2,1)} %bitcast.62), kind=kLoop, calls=%fused_computation.92 | loop fusion | bytes 20971520 | tf_op jit(solution)/shard_map/slice | solution.py:64
  101.7 8.6 %copy.35 = bf16[32,128,640]{1,0,2:T(8,128)(2,1)} copy(bf16[32,128,640]{2,1,0:T(8,128)(2,1)} %get-tuple-element.27) | data formatting | bytes 10485760 | tf_op jit(solution)/shard_map/slice | solution.py:64
  110.3 8.8 %reshape_reshape.6 = bf16[4096,10,64]{0,2,1:T(8,128)(2,1)} reshape(bf16[32,128,640]{1,0,2:T(8,128)(2,1)} %copy.35) | data formatting | bytes 10485760 | tf_op jit(solution)/shard_map/reshape;reshape | solution.py:70
  119.1 8.6 %copy.36 = bf16[32,128,640]{1,0,2:T(8,128)(2,1)} copy(bf16[32,128,640]{2,1,0:T(8,128)(2,1)} %get-tuple-element.28) | data formatting | bytes 10485760 | tf_op jit(solution)/shard_map/slice | solution.py:65
  127.7 8.8 %reshape_reshape.7 = bf16[4096,10,64]{0,2,1:T(8,128)(2,1)} reshape(bf16[32,128,640]{1,0,2:T(8,128)(2,1)} %copy.36) | data formatting | bytes 10485760 | tf_op jit(solution)/shard_map/reshape;reshape | solution.py:71
  137.0 19.1 %fusion.53 = (f32[10,128]{1,0:T(8,128)S(1)}, bf16[10,128,4096]{2,1,0:T(8,128)(2,1)}) fusion(pred[128,4096]{1,0:T(8,128)(4,1)S(1)} %fusion.12, bf16[4096,10,64]{0,2,1:T(8,128)(2,1)} %reshape_reshape.6, f32[128,10,64]{0,2,1:T(8,128)S(1)} %bitcast.65, f32[10,64]{1,0:T(8,128)S(1)} %mul.184, f32[128,10]{0,1:T(8,128)S(1)} %add_rsqrt_fusion), kind=kOutput, calls=%fused_computation.95 | convolution fusion | flops 1379373056 | bytes 16593408 | tf_op jit(solution)/shard_map/sub | solution.py:78
  156.1 9.3 %fusion.19 = bf16[128,10,64]{0,2,1:T(8,128)(2,1)S(1)} fusion(bf16[4096,10,64]{0,2,1:T(8,128)(2,1)} %reshape_reshape.7, bf16[10,128,4096]{2,1,0:T(8,128)(2,1)} %get-tuple-element.34, f32[128,10]{0,1:T(8,128)S(1)} %bitcast.76), kind=kOutput, calls=%fused_computation.18 | convolution fusion | flops 671252480 | bytes 15897600 | tf_op jit(solution)/shard_map/hqk,khd->hqd/dot_general | solution.py:80
  166.7 1.0 multiply_convert_fusion.2
  167.9 81.0 %all-gather.8.cloned.1.call-done = bf16[1024,1280]{1,0:T(8,128)(2,1)} async-done(((bf16[128,1280]{1,0:T(8,128)(2,1)}), bf16[1024,1280]{1,0:T(8,128)(2,1)}) %all-gather.8.cloned.1.call-update) | async-done | bytes 2621456 | tf_op jit(solution)/shard_map/all_gather | solution.py:95
  249.0 5.9 %fusion.54 = f32[1024,640]{1,0:T(8,128)} fusion(bf16[1024,1280]{1,0:T(8,128)(2,1)} %all-gather.8.cloned.1.call-done, bf16[1280,640]{1,0:T(8,128)(2,1)} %param.26), kind=kOutput, calls=%fused_computation.96 | convolution fusion | flops 1677721600 | bytes 6881280 | tf_op jit(solution)/shard_map/dot_general | solution.py:96
  254.9 8.9 %convolution_convert_fusion = bf16[1024,1280]{1,0:T(8,128)(2,1)} fusion(bf16[640,1280]{1,0:T(8,128)(2,1)S(1)} %copy-done, f32[1024,640]{1,0:T(8,128)} %fusion.54, bf16[1024,1280]{1,0:T(8,128)(2,1)} %all-gather.8.cloned.1.call-done, bf16[1280,640]{1,0:T(8,128)(2,1)} %param.27, f32[640]{0:T(1024)S(1)} %copy-done.10, f32[640]{0:T(1024)S(1)} %copy-done.11), kind=kOutput, calls=%fused_computation.11 | convolution fusion | flops 3361996800 | bytes 11146240 | tf_op jit(solution)/shard_map/dot_general | solution.py:100
  264.4 96.8 %reduce-scatter.2.cloned.1.call-done = bf16[128,1280]{1,0:T(8,128)(2,1)} async-done(((bf16[1024,1280]{1,0:T(8,128)(2,1)}), bf16[128,1280]{1,0:T(8,128)(2,1)}) %reduce-scatter.2.cloned.1.call-update) | async-done | bytes 327696 | tf_op jit(solution)/shard_map/reduce_scatter | solution.py:99
  361.2 1.1 fusion.26
  362.3 1.3 multiply_reduce_fusion
  363.6 1.4 multiply_convert_fusion.1
  366.7 56.6 %all-gather.12.cloned.1.call-done = f32[256,1280]{1,0:T(8,128)} async-done(((f32[8,1280]{1,0:T(8,128)}), f32[256,1280]{1,0:T(8,128)}) %all-gather.12.cloned.1.call-update) | async-done | bytes 1310736 | tf_op jit(solution)/shard_map/all_gather | solution.py:120
  423.3 1.4 bitcast_reduce_fusion
  425.6 38.8 %all-gather.3 = f32[8,5,1280]{2,1,0:T(8,128)S(1)} all-gather(f32[1,5,1280]{2,1,0:T(8,128)S(1)} %fusion.30), channel_id=4, replica_groups=mesh['dp'=8,'tensor'=32] {'dp'}, dimensions={0}, use_global_device_ids=true | all-gather | bytes 230400 | tf_op jit(solution)/shard_map/all_gather | solution.py:127
  464.9 81.3 %pmax.7 = f32[32]{0:T(128)S(1)} all-reduce(f32[32]{0:T(128)S(1)} %fusion.22), channel_id=1, replica_groups=mesh['dp'=8,'tensor'=32] {'dp','tensor'}, use_global_device_ids=true, to_apply=%region_17.18 | all-reduce | flops 32 | bytes 256 | tf_op jit(solution)/shard_map/pmax | solution.py:135
  (79 shorter events, 8.0 us)
Async XLA Ops:
  7.2 247.7 %copy-start = (bf16[640,1280]{1,0:T(8,128)(2,1)S(1)}, bf16[640,1280]{1,0:T(8,128)(2,1)}, u32[]{:S(2)}) copy-start(bf16[640,1280]{1,0:T(8,128)(2,1)} %param.30) | copy-start | bytes 4915204
  7.2 84.0 %all-gather.10.cloned.1.call-start = ((), (), s32[]{:S(2)}) async-start(), calls=%async_computation.3 | async-start | bytes 11489280 | tf_op jit(solution)/shard_map/all_gather | solution.py:63
  8.5 3.5 copy-start.9
  11.9 0.7 copy-start.8
  13.4 235.5 %all-gather.8.cloned.1.call-start = ((), (), s32[]{:S(2)}) async-start(), calls=%async_computation.1 | async-start | bytes 2949120 | tf_op jit(solution)/shard_map/all_gather | solution.py:95
  156.1 9.3 %copy-start.4 = (bf16[640,1280]{1,0:T(8,128)(2,1)S(1)}, bf16[640,1280]{1,0:T(8,128)(2,1)}, u32[]{:S(2)}) copy-start(bf16[640,1280]{1,0:T(8,128)(2,1)} %param.24) | copy-start | bytes 4915204
  156.1 9.9 %copy-start.6 = (f32[1280]{0:T(1024)S(1)}, f32[1280]{0:T(1024)}, u32[]{:S(2)}) copy-start(f32[1280]{0:T(1024)} %param.25) | copy-start | bytes 15364
  165.4 1.0 copy-start.1
  167.7 87.2 %copy-start.10 = (f32[640]{0:T(1024)S(1)}, f32[640]{0:T(1024)}, u32[]{:S(2)}) copy-start(f32[640]{0:T(1024)} %param.29) | copy-start | bytes 7684
  167.7 87.2 %copy-start.11 = (f32[640]{0:T(1024)S(1)}, f32[640]{0:T(1024)}, u32[]{:S(2)}) copy-start(f32[640]{0:T(1024)} %param.28) | copy-start | bytes 7684
  167.7 193.5 %reduce-scatter.2.cloned.1.call-start = ((), (), s32[]{:S(2)}) async-start(), calls=%async_computation.2 | async-start | bytes 2949120 | tf_op jit(solution)/shard_map/reduce_scatter | solution.py:99
  263.8 98.5 %copy-start.2 = (bf16[128,1280]{1,0:T(8,128)(2,1)S(1)}, bf16[128,1280]{1,0:T(8,128)(2,1)}, u32[]{:S(2)}) copy-start(bf16[128,1280]{1,0:T(8,128)(2,1)} %multiply_convert_fusion.2) | copy-start | bytes 983044
  263.8 98.5 %copy-start.7 = (f32[1280]{0:T(1024)S(1)}, f32[1280]{0:T(1024)}, u32[]{:S(2)}) copy-start(f32[1280]{0:T(1024)} %param.31) | copy-start | bytes 15364
  263.8 102.3 %copy-start.12 = (bf16[125]{0:T(256)(128)(2,1)S(1)}, bf16[125]{0:T(256)(128)(2,1)}, u32[]{:S(2)}) copy-start(bf16[125]{0:T(256)(128)(2,1)} %param.33) | copy-start | bytes 754
  263.9 200.7 %copy-start.5 = (bf16[1280,125]{1,0:T(8,128)(2,1)S(1)}, bf16[1280,125]{1,0:T(8,128)(2,1)}, u32[]{:S(2)}) copy-start(bf16[1280,125]{1,0:T(8,128)(2,1)} %param.32) | copy-start | bytes 960004
  263.9 159.5 %all-gather.12.cloned.1.call-start = ((), (), s32[]{:S(2)}) async-start(), calls=%async_computation.4 | async-start | bytes 1351680 | tf_op jit(solution)/shard_map/all_gather | solution.py:120
  362.3 183.9 %copy-start.13 = (s32[32]{0:T(128)S(1)}, s32[32]{0:T(128)}, u32[]{:S(2)}) copy-start(s32[32]{0:T(128)} %param.21) | copy-start | bytes 388
  365.0 182.6 %copy-start.3 = (bf16[128,1280]{1,0:T(8,128)(2,1)}, bf16[128,1280]{1,0:T(8,128)(2,1)S(1)}, u32[]{:S(2)}) copy-start(bf16[128,1280]{1,0:T(8,128)(2,1)S(1)} %multiply_convert_fusion.1) | copy-start | bytes 983044
Sparse Core Ops, SparseCore 0:
  13.6 77.5 all-gather.9
  167.8 81.1 all-gather.7
  264.0 97.1 reduce-scatter.1
  366.2 57.0 all-gather.11

commit v3 on v2

--- a/solution.py
+++ b/solution.py
@@ -67,28 +67,35 @@
     tally = jnp.sum((seg_all[:, None] == request_numbers[None, :]).astype(jnp.int32), axis=0)
     total_keys = key_all.shape[0]
     key_pos = jnp.arange(total_keys, dtype=jnp.int32)
-    key_heads = key_all.reshape(total_keys, HEADS, HD)
-    value_heads = value_all.reshape(total_keys, HEADS, HD)
+    head_of_column = jnp.arange(head_width, dtype=jnp.int32) // HD
+    head_mask = (jnp.arange(HEADS, dtype=jnp.int32)[:, None] == head_of_column[None, :]).astype(
+        jnp.bfloat16
+    )
+    query_flat = queries.reshape(row_count, head_width)
+    query_blocks = (query_flat[None, :, :] * head_mask[:, None, :]).reshape(
+        HEADS * row_count, head_width
+    )
     scores = (
-        jnp.einsum("qhd,khd->hqk", queries, key_heads, preferred_element_type=jnp.float32)
+        lax.dot_general(
+            query_blocks,
+            key_all,
+            (((1,), (1,)), ((), ())),
+            preferred_element_type=jnp.float32,
+        ).reshape(HEADS, row_count, total_keys)
         * score_scale
     )
     allowed = (seg_all[None, :] == segments[:, None]) & (key_pos[None, :] <= positions[:, None])
     row_max = jnp.max(jnp.where(allowed[None], scores, NEGATIVE), axis=2)
     weights = jnp.where(allowed[None], jnp.exp(scores - row_max[:, :, None]), 0.0)
     weight_sum = jnp.sum(weights, axis=2)
-    weighted = jnp.einsum(
-        "hqk,khd->hqd",
-        weights.astype(jnp.bfloat16),
-        value_heads,
+    weighted = jnp.dot(
+        weights.astype(jnp.bfloat16).reshape(HEADS * row_count, total_keys),
+        value_all,
         preferred_element_type=jnp.float32,
-    )
-    attended = (
-        (weighted / weight_sum[:, :, None])
-        .transpose(1, 0, 2)
-        .reshape(row_count, head_width)
-        .astype(jnp.bfloat16)
-    )
+    ).reshape(HEADS, row_count, head_width)
+    attended = jnp.sum(
+        (weighted / weight_sum[:, :, None]) * head_mask[:, None, :].astype(jnp.float32), axis=0
+    ).astype(jnp.bfloat16)
     attn_rows = normalize(jnp.dot(attended, w_out, preferred_element_type=jnp.float32))
     residual_in = start_rows.astype(jnp.float32)
     mid_rows = normalize(residual_in + alpha_attn * (attn_rows - residual_in)).astype(jnp.bfloat16)

time: 555 us -> 553 us (level)
  local copies, waits for them, and re-layouts: 45.8 us -> 12.2 us
  other arithmetic: 12.6 us -> 35.9 us
  matrix products: 49.3 us -> 57.5 us
    dot_general x1 -> x2, matrix products: 9.29 us -> 35.2 us  [the longest x1 21 us: local(): jnp.dot(weights.astype(jnp.bfloat16).reshape(HEADS * row_count, total_key...]
    sub x0 -> x1, other arithmetic: none -> 21.3 us  [local(): scores - row_max[:, :, None]]
    sub x1 -> x0, matrix products: 19.1 us -> none  [local(): scores - row_max[:, :, None]]
    another operation x2 -> x0, local copies, waits for them, and re-layouts: 17.6 us -> none  [the longest x1 8.82 us: local(): value_heads = value_all.reshape(total_keys, HEADS, HD)]
    slice x2 -> x0, local copies, waits for them, and re-layouts: 8.74 us -> none  [the longest x1 8.58 us: local(): value_all = gathered[:, :row_count, head_width:].reshape(-1, head_width)]
    slice x2 -> x1, local copies, waits for them, and re-layouts: 18.2 us -> 9.76 us  [local(): key_all = gathered[:, :row_count, :head_width].reshape(-1, head_width)]
where the time goes in v3:
time: 553 us; the launch traced here: 552 us
  waiting for transfers between devices  312 us (56%)
  blocking collectives  120 us (22%)
  matrix products  57.5 us (10%)
  other arithmetic  35.9 us (6%)
  between operations  14.1 us (3%)
  local copies, waits for them, and re-layouts  12.2 us (2%)
    reduce_scatter x1, waiting for transfers between devices, local(): lax.psum_scatter(jnp.dot(hidden, w_down, preferred_element_type=jnp.float...  97 us
    pmax x1, blocking collectives, local(): every_max = lax.pmax(jnp.max(logits, axis=1), ('dp', 'tensor'))  81.3 us
    all_gather x1, waiting for transfers between devices, local(): received = lax.all_gather(mid_rows, 'dp', axis=0, tiled=True)  81.2 us
    all_gather x1, waiting for transfers between devices, local(): gathered = lax.all_gather(packed, 'tensor', axis=0, tiled=False)  77.7 us
    all_gather x1, waiting for transfers between devices, local(): lax.all_gather(partial, 'tensor', axis=0, tiled=False)  56.5 us
    all_gather x1, blocking collectives, local(): lax.all_gather(jnp.concatenate([last_rows, norm_row], axis=0), 'dp', axis...  38.8 us
    sub x1, other arithmetic, local(): scores - row_max[:, :, None]  21.3 us
    dot_general x1, matrix products, local(): jnp.dot(weights.astype(jnp.bfloat16).reshape(HEADS * row_count, total_key...  21 us
  transfers between devices with their start and end apart: 4, of which 4 were waited for; matrix products, arithmetic and copies ran while one was open for 0% of the time, Pallas kernels for 0%

profile of v3, /device:TPU:1, one launch (start us, length us, event | category | flops | bytes accessed | tf_op | source)
XLA Modules:
  0.0 552.3 jit_solution(6860638837858093574)
XLA Ops:
  7.2 1.2 fusion.22
  8.5 3.4 fusion.59
  12.0 0.9 copy.28
  12.9 1.0 reduce_sum.119
  14.0 0.9 copy.29
  15.3 1.0 multiply_convert_fusion.3
  17.2 77.7 %all-gather.10.cloned.1.call-done = bf16[4352,1280]{1,0:T(8,128)(2,1)} async-done(((bf16[136,1280]{1,0:T(8,128)(2,1)}), bf16[4352,1280]{1,0:T(8,128)(2,1)}) %all-gather.10.cloned.1.call-update) | async-done | bytes 11141136 | tf_op jit(solution)/shard_map/all_gather | solution.py:63
  95.7 9.8 %fusion.61 = (bf16[32,128,640]{2,1,0:T(8,128)(2,1)}, bf16[32,128,640]{2,1,0:T(8,128)(2,1)}) fusion(bf16[32,136,1280]{2,1,0:T(8,128)(2,1)} %bitcast.55), kind=kLoop, calls=%fused_computation.108 | loop fusion | bytes 20971520 | tf_op jit(solution)/shard_map/slice | solution.py:64
  106.0 14.1 %fusion.13 = f32[10,128,4096]{2,1,0:T(8,128)} fusion(bf16[4096,640,1]{1,0,2:T(8,128)(2,1)} %bitcast.57, bf16[10,640]{1,0:T(8,128)(2,1)S(1)} %get-tuple-element.35, bf16[128,640]{1,0:T(8,128)(2,1)S(1)} %get-tuple-element.29), kind=kOutput, calls=%fused_computation.15 | convolution fusion | flops 6711705600 | bytes 26391040 | tf_op jit(solution)/shard_map/dot_general | solution.py:79
  120.1 21.3 %fusion.63 = f32[10,128]{1,0:T(8,128)S(1)} fusion(f32[10,128,4096]{2,1,0:T(8,128)} %fusion.13, pred[128,4096]{1,0:T(8,128)(4,1)S(1)} %fusion.10), kind=kOutput, calls=%fused_computation.110 | output fusion | flops 31461376 | bytes 21500928 | tf_op jit(solution)/shard_map/sub | solution.py:89
  141.4 21.0 %multiply_reduce_fusion = bf16[128,640]{1,0:T(8,128)(2,1)S(1)} fusion(bf16[4096,640,1]{1,0,2:T(8,128)(2,1)} %bitcast.56, f32[10,640]{1,0:T(8,128)S(1)} %get-tuple-element.36, f32[10,128]{1,0:T(8,128)S(1)} %fusion.63, f32[10,128,4096]{2,1,0:T(8,128)} %fusion.13, pred[128,4096]{1,0:T(8,128)(4,1)S(1)} %fusion.10), kind=kOutput, calls=%fused_computation.11 | convolution fusion | flops 6744724480 | bytes 26933248 | tf_op jit(solution)/shard_map/dot_general | solution.py:91
  162.5 1.9 multiply_reduce_fusion.3
  164.8 1.0 multiply_convert_fusion.2
  165.9 81.2 %all-gather.8.cloned.1.call-done = bf16[1024,1280]{1,0:T(8,128)(2,1)} async-done(((bf16[128,1280]{1,0:T(8,128)(2,1)}), bf16[1024,1280]{1,0:T(8,128)(2,1)}) %all-gather.8.cloned.1.call-update) | async-done | bytes 2621456 | tf_op jit(solution)/shard_map/all_gather | solution.py:102
  247.1 5.9 %fusion.64 = f32[1024,640]{1,0:T(8,128)} fusion(bf16[1024,1280]{1,0:T(8,128)(2,1)} %all-gather.8.cloned.1.call-done, bf16[1280,640]{1,0:T(8,128)(2,1)} %param.26), kind=kOutput, calls=%fused_computation.111 | convolution fusion | flops 1677721600 | bytes 6881280 | tf_op jit(solution)/shard_map/dot_general | solution.py:103
  253.0 9.0 %convolution_convert_fusion = bf16[1024,1280]{1,0:T(8,128)(2,1)} fusion(bf16[640,1280]{1,0:T(8,128)(2,1)S(1)} %copy-done, f32[1024,640]{1,0:T(8,128)} %fusion.64, bf16[1024,1280]{1,0:T(8,128)(2,1)} %all-gather.8.cloned.1.call-done, bf16[1280,640]{1,0:T(8,128)(2,1)} %param.27, f32[640]{0:T(1024)S(1)} %copy-done.9, f32[640]{0:T(1024)S(1)} %copy-done.10), kind=kOutput, calls=%fused_computation.10 | convolution fusion | flops 3361996800 | bytes 11146240 | tf_op jit(solution)/shard_map/dot_general | solution.py:107
  262.5 97.0 %reduce-scatter.2.cloned.1.call-done = bf16[128,1280]{1,0:T(8,128)(2,1)} async-done(((bf16[1024,1280]{1,0:T(8,128)(2,1)}), bf16[128,1280]{1,0:T(8,128)(2,1)}) %reduce-scatter.2.cloned.1.call-update) | async-done | bytes 327696 | tf_op jit(solution)/shard_map/reduce_scatter | solution.py:106
  359.5 1.1 fusion.21
  360.6 1.3 multiply_reduce_fusion.1
  361.9 1.4 multiply_convert_fusion.1
  365.0 56.5 %all-gather.12.cloned.1.call-done = f32[256,1280]{1,0:T(8,128)} async-done(((f32[8,1280]{1,0:T(8,128)}), f32[256,1280]{1,0:T(8,128)}) %all-gather.12.cloned.1.call-update) | async-done | bytes 1310736 | tf_op jit(solution)/shard_map/all_gather | solution.py:127
  421.5 1.4 bitcast_reduce_fusion
  423.8 38.8 %all-gather.3 = f32[8,5,1280]{2,1,0:T(8,128)S(1)} all-gather(f32[1,5,1280]{2,1,0:T(8,128)S(1)} %fusion.31), channel_id=4, replica_groups=mesh['dp'=8,'tensor'=32] {'dp'}, dimensions={0}, use_global_device_ids=true | all-gather | bytes 230400 | tf_op jit(solution)/shard_map/all_gather | solution.py:134
  463.1 81.3 %pmax.7 = f32[32]{0:T(128)S(1)} all-reduce(f32[32]{0:T(128)S(1)} %fusion.15), channel_id=1, replica_groups=mesh['dp'=8,'tensor'=32] {'dp','tensor'}, use_global_device_ids=true, to_apply=%region_18.19 | all-reduce | flops 32 | bytes 256 | tf_op jit(solution)/shard_map/pmax | solution.py:142
  (77 shorter events, 8.1 us)
Async XLA Ops:
  7.2 245.8 %copy-start = (bf16[640,1280]{1,0:T(8,128)(2,1)S(1)}, bf16[640,1280]{1,0:T(8,128)(2,1)}, u32[]{:S(2)}) copy-start(bf16[640,1280]{1,0:T(8,128)(2,1)} %param.30) | copy-start | bytes 4915204
  7.2 87.7 %all-gather.10.cloned.1.call-start = ((), (), s32[]{:S(2)}) async-start(), calls=%async_computation.3 | async-start | bytes 11489280 | tf_op jit(solution)/shard_map/all_gather | solution.py:63
  8.5 3.5 copy-start.7
  11.9 3.4 copy-start.8
  17.1 229.9 %all-gather.8.cloned.1.call-start = ((), (), s32[]{:S(2)}) async-start(), calls=%async_computation.1 | async-start | bytes 2949120 | tf_op jit(solution)/shard_map/all_gather | solution.py:102
  141.4 23.0 %copy-start.1 = (bf16[1,128,1280]{2,1,0:T(8,128)(2,1)S(1)}, bf16[1,128,1280]{2,1,0:T(8,128)(2,1)}, u32[]{:S(2)}) copy-start(bf16[1,128,1280]{2,1,0:T(8,128)(2,1)} %param.19) | copy-start | bytes 983044
  141.4 23.0 %copy-start.5 = (f32[1280]{0:T(1024)S(1)}, f32[1280]{0:T(1024)}, u32[]{:S(2)}) copy-start(f32[1280]{0:T(1024)} %param.25) | copy-start | bytes 15364
  165.8 87.2 %copy-start.9 = (f32[640]{0:T(1024)S(1)}, f32[640]{0:T(1024)}, u32[]{:S(2)}) copy-start(f32[640]{0:T(1024)} %param.29) | copy-start | bytes 7684
  165.8 87.2 %copy-start.10 = (f32[640]{0:T(1024)S(1)}, f32[640]{0:T(1024)}, u32[]{:S(2)}) copy-start(f32[640]{0:T(1024)} %param.28) | copy-start | bytes 7684
  165.8 193.6 %reduce-scatter.2.cloned.1.call-start = ((), (), s32[]{:S(2)}) async-start(), calls=%async_computation.2 | async-start | bytes 2949120 | tf_op jit(solution)/shard_map/reduce_scatter | solution.py:106
  253.0 107.6 %copy-start.2 = (bf16[128,1280]{1,0:T(8,128)(2,1)S(1)}, bf16[128,1280]{1,0:T(8,128)(2,1)}, u32[]{:S(2)}) copy-start(bf16[128,1280]{1,0:T(8,128)(2,1)} %multiply_convert_fusion.2) | copy-start | bytes 983044
  253.0 107.6 %copy-start.6 = (f32[1280]{0:T(1024)S(1)}, f32[1280]{0:T(1024)}, u32[]{:S(2)}) copy-start(f32[1280]{0:T(1024)} %param.31) | copy-start | bytes 15364
  262.0 102.4 %copy-start.11 = (bf16[125]{0:T(256)(128)(2,1)S(1)}, bf16[125]{0:T(256)(128)(2,1)}, u32[]{:S(2)}) copy-start(bf16[125]{0:T(256)(128)(2,1)} %param.33) | copy-start | bytes 754
  262.0 200.8 %copy-start.4 = (bf16[1280,125]{1,0:T(8,128)(2,1)S(1)}, bf16[1280,125]{1,0:T(8,128)(2,1)}, u32[]{:S(2)}) copy-start(bf16[1280,125]{1,0:T(8,128)(2,1)} %param.32) | copy-start | bytes 960004
  262.0 282.4 %copy-start.12 = (s32[32]{0:T(128)S(1)}, s32[32]{0:T(128)}, u32[]{:S(2)}) copy-start(s32[32]{0:T(128)} %param.21) | copy-start | bytes 388
  262.0 159.5 %all-gather.12.cloned.1.call-start = ((), (), s32[]{:S(2)}) async-start(), calls=%async_computation.4 | async-start | bytes 1351680 | tf_op jit(solution)/shard_map/all_gather | solution.py:127
  363.3 182.5 %copy-start.3 = (bf16[128,1280]{1,0:T(8,128)(2,1)}, bf16[128,1280]{1,0:T(8,128)(2,1)S(1)}, u32[]{:S(2)}) copy-start(bf16[128,1280]{1,0:T(8,128)(2,1)S(1)} %multiply_convert_fusion.1) | copy-start | bytes 983044
Sparse Core Ops, SparseCore 0:
  17.2 77.5 all-gather.9
  165.9 81.1 all-gather.7
  262.1 97.2 reduce-scatter.1
  364.5 57.0 all-gather.11

commit v4 on v3

--- a/solution.py
+++ b/solution.py
@@ -61,6 +61,11 @@
         [jnp.concatenate([key_rows, value_rows], axis=1), seg_block], axis=0
     )
     gathered = lax.all_gather(packed, "tensor", axis=0, tiled=False)
+    vocab_pack = jnp.concatenate(
+        [w_vocab, logit_gain[None], jnp.zeros((7, w_vocab.shape[1]), w_vocab.dtype)], axis=0
+    )
+    vocab_pack, gathered = lax.optimization_barrier((vocab_pack, gathered))
+    vocab_all = lax.all_gather(vocab_pack, "dp", axis=0, tiled=False)
     key_all = gathered[:, :row_count, :head_width].reshape(-1, head_width)
     value_all = gathered[:, :row_count, head_width:].reshape(-1, head_width)
     seg_all = gathered[:, row_count, :row_count].reshape(-1).astype(jnp.int32)
@@ -99,6 +104,7 @@
     attn_rows = normalize(jnp.dot(attended, w_out, preferred_element_type=jnp.float32))
     residual_in = start_rows.astype(jnp.float32)
     mid_rows = normalize(residual_in + alpha_attn * (attn_rows - residual_in)).astype(jnp.bfloat16)
+    mid_rows, vocab_all = lax.optimization_barrier((mid_rows, vocab_all))
     received = lax.all_gather(mid_rows, "dp", axis=0, tiled=True)
     up_proj = jnp.dot(received, w_up, preferred_element_type=jnp.float32) * up_gain
     gate_proj = jnp.dot(received, w_gate, preferred_element_type=jnp.float32) * gate_gain
@@ -130,16 +136,20 @@
     request_mean = row_sums / counts[:, None]
     group_norm = jnp.sqrt(jnp.mean(request_mean * request_mean, axis=1))
     slot_count = lax.axis_size("dp") * REQS
-    norm_row = jnp.zeros((1, last_rows.shape[1]), jnp.float32).at[0, :REQS].set(group_norm)
-    pack_stats = lax.all_gather(
-        jnp.concatenate([last_rows, norm_row], axis=0), "dp", axis=0, tiled=False
-    )
-    every_last = pack_stats[:, :REQS].reshape(slot_count, -1)
-    every_norm = pack_stats[:, REQS, :REQS].reshape(slot_count)
-    logits = jnp.dot(
-        every_last.astype(jnp.bfloat16), w_vocab, preferred_element_type=jnp.float32
-    ) * logit_gain.astype(jnp.float32)
-    every_max = lax.pmax(jnp.max(logits, axis=1), ("dp", "tensor"))
+    dp_index = lax.axis_index("dp")
+    model_width = last_rows.shape[1]
+    pack_logits = jnp.einsum(
+        "rd,gdc->rgc",
+        last_rows.astype(jnp.bfloat16),
+        vocab_all[:, :model_width],
+        preferred_element_type=jnp.float32,
+    ) * vocab_all[None, :, model_width].astype(jnp.float32)
+    pack_max = jnp.max(pack_logits.reshape(REQS, -1), axis=1)
+    own_slot = jnp.arange(slot_count, dtype=jnp.int32) // REQS == dp_index
+    spread_max = jnp.where(own_slot, jnp.tile(pack_max, slot_count // REQS), NEGATIVE)
+    spread_norm = jnp.where(own_slot, jnp.tile(group_norm, slot_count // REQS), NEGATIVE)
+    every = lax.pmax(jnp.concatenate([spread_max, spread_norm]), ("dp", "tensor"))
+    every_max, every_norm = every[:slot_count], every[slot_count:]
     placement = (pack_of_group[:, None] == jnp.arange(slot_count, dtype=jnp.int32)[None, :]).astype(
         jnp.float32
     )

time: 553 us -> 532 us (0.962)
  blocking collectives: 120 us -> 76.1 us
  waiting for transfers between devices: 312 us -> 328 us
    all_gather x1 -> x0, blocking collectives: 38.8 us -> none  [local(): lax.all_gather(jnp.concatenate([last_rows, norm_row], axis=0), 'dp', axis...]
    all_gather x0 -> x1, waiting for transfers between devices: none -> 17.6 us  [local(): vocab_all = lax.all_gather(vocab_pack, 'dp', axis=0, tiled=False)]
  transfers between devices with their start and end apart: 4 -> 5, of which waited for: 4 -> 5; matrix products, arithmetic and copies ran while one was open for 0% -> 13% of each run, Pallas kernels for 0% -> 0%
where the time goes in v4:
time: 532 us; the launch traced here: 531 us
  waiting for transfers between devices  328 us (62%)
  blocking collectives  76.1 us (14%)
  matrix products  61.9 us (12%)
  other arithmetic  35.4 us (7%)
  local copies, waits for them, and re-layouts  15.7 us (3%)
  between operations  14.1 us (3%)
    reduce_scatter x1, waiting for transfers between devices, local(): lax.psum_scatter(jnp.dot(hidden, w_down, preferred_element_type=jnp.float...  96.8 us
    all_gather x1, waiting for transfers between devices, local(): received = lax.all_gather(mid_rows, 'dp', axis=0, tiled=True)  82.3 us
    pmax x1, blocking collectives, local(): lax.pmax(jnp.concatenate([spread_max, spread_norm]), ('dp', 'tensor'))  76.1 us
    all_gather x1, waiting for transfers between devices, local(): gathered = lax.all_gather(packed, 'tensor', axis=0, tiled=False)  74.5 us
    all_gather x1, waiting for transfers between devices, local(): lax.all_gather(partial, 'tensor', axis=0, tiled=False)  56.5 us
    dot_general x1, matrix products, local(): jnp.dot(weights.astype(jnp.bfloat16).reshape(HEADS * row_count, total_key...  25.4 us
    sub x1, other arithmetic, local(): scores - row_max[:, :, None]  21.3 us
    all_gather x1, waiting for transfers between devices, local(): vocab_all = lax.all_gather(vocab_pack, 'dp', axis=0, tiled=False)  17.6 us
  transfers between devices with their start and end apart: 5, of which 5 were waited for; matrix products, arithmetic and copies ran while one was open for 13% of the time, Pallas kernels for 0%

profile of v4, /device:TPU:1, one launch (start us, length us, event | category | flops | bytes accessed | tf_op | source)
XLA Modules:
  0.0 531.5 jit_solution(686103989339924962)
XLA Ops:
  7.2 1.2 fusion.29
  8.5 3.4 fusion.65
  12.0 0.9 copy.24
  12.9 1.0 reduce_sum.119
  15.3 1.0 multiply_convert_fusion.3
  17.2 3.1 concatenate.17
  20.3 74.5 %all-gather.10.cloned.1.call-done = bf16[4352,1280]{1,0:T(8,128)(2,1)} async-done(((bf16[136,1280]{1,0:T(8,128)(2,1)}), bf16[4352,1280]{1,0:T(8,128)(2,1)}) %all-gather.10.cloned.1.call-update) | async-done | bytes 11141136 | tf_op jit(solution)/shard_map/all_gather | solution.py:63
  95.7 9.8 %fusion.67 = (bf16[32,128,640]{2,1,0:T(8,128)(2,1)}, bf16[32,128,640]{2,1,0:T(8,128)(2,1)}) fusion(bf16[32,136,1280]{2,1,0:T(8,128)(2,1)} %bitcast.57), kind=kLoop, calls=%fused_computation.114 | loop fusion | bytes 20971520 | tf_op jit(solution)/shard_map/slice | solution.py:69
  106.3 14.1 %fusion.15 = f32[10,128,4096]{2,1,0:T(8,128)} fusion(bf16[4096,640,1]{1,0,2:T(8,128)(2,1)} %bitcast.59, bf16[10,640]{1,0:T(8,128)(2,1)S(1)} %get-tuple-element.29, bf16[128,640]{1,0:T(8,128)(2,1)S(1)} %get-tuple-element.25), kind=kOutput, calls=%fused_computation.17 | convolution fusion | flops 6711705600 | bytes 26391040 | tf_op jit(solution)/shard_map/dot_general | solution.py:84
  120.4 21.3 %fusion.68 = f32[10,128]{1,0:T(8,128)S(1)} fusion(f32[10,128,4096]{2,1,0:T(8,128)} %fusion.15, pred[128,4096]{1,0:T(8,128)(4,1)S(1)} %fusion.12), kind=kOutput, calls=%fused_computation.115 | output fusion | flops 31461376 | bytes 21500928 | tf_op jit(solution)/shard_map/sub | solution.py:94
  141.7 25.4 %multiply_reduce_fusion = bf16[128,640]{1,0:T(8,128)(2,1)S(1)} fusion(bf16[4096,640,1]{1,0,2:T(8,128)(2,1)} %bitcast.58, f32[10,640]{1,0:T(8,128)S(1)} %get-tuple-element.30, f32[10,128]{1,0:T(8,128)S(1)} %fusion.68, f32[10,128,4096]{2,1,0:T(8,128)} %fusion.15, pred[128,4096]{1,0:T(8,128)(4,1)} %copy-done.5), kind=kOutput, calls=%fused_computation.11 | convolution fusion | flops 6744724480 | bytes 26933248 | tf_op jit(solution)/shard_map/dot_general | solution.py:96
  168.4 1.0 multiply_convert_fusion.2
  169.4 17.6 %all-gather.12.cloned.1.call-done = bf16[10304,125]{1,0:T(8,128)(2,1)} async-done(((bf16[1288,125]{1,0:T(8,128)(2,1)}), bf16[10304,125]{1,0:T(8,128)(2,1)}) %all-gather.12.cloned.1.call-update) | async-done | bytes 2576016 | tf_op jit(solution)/shard_map/all_gather | solution.py:68
  187.1 82.3 %all-gather.8.cloned.1.call-done = bf16[1024,1280]{1,0:T(8,128)(2,1)} async-done(((bf16[128,1280]{1,0:T(8,128)(2,1)}), bf16[1024,1280]{1,0:T(8,128)(2,1)}) %all-gather.8.cloned.1.call-update) | async-done | bytes 2621456 | tf_op jit(solution)/shard_map/all_gather | solution.py:108
  269.4 5.4 %fusion.69 = f32[1024,640]{1,0:T(8,128)} fusion(bf16[1024,1280]{1,0:T(8,128)(2,1)} %all-gather.8.cloned.1.call-done, bf16[1280,640]{1,0:T(8,128)(2,1)S(1)} %copy-done.11), kind=kOutput, calls=%fused_computation.116 | convolution fusion | flops 1677721600 | bytes 6881280 | tf_op jit(solution)/shard_map/dot_general | solution.py:109
  274.8 8.9 %convolution_convert_fusion = bf16[1024,1280]{1,0:T(8,128)(2,1)} fusion(bf16[640,1280]{1,0:T(8,128)(2,1)S(1)} %copy-done, f32[1024,640]{1,0:T(8,128)} %fusion.69, bf16[1024,1280]{1,0:T(8,128)(2,1)} %all-gather.8.cloned.1.call-done, bf16[1280,640]{1,0:T(8,128)(2,1)} %param.25, f32[640]{0:T(1024)S(1)} %copy-done.12, f32[640]{0:T(1024)S(1)} %copy-done.13), kind=kOutput, calls=%fused_computation.10 | convolution fusion | flops 3361996800 | bytes 11146240 | tf_op jit(solution)/shard_map/dot_general | solution.py:113
  284.3 96.8 %reduce-scatter.2.cloned.1.call-done = bf16[128,1280]{1,0:T(8,128)(2,1)} async-done(((bf16[1024,1280]{1,0:T(8,128)(2,1)}), bf16[128,1280]{1,0:T(8,128)(2,1)}) %reduce-scatter.2.cloned.1.call-update) | async-done | bytes 327696 | tf_op jit(solution)/shard_map/reduce_scatter | solution.py:112
  381.1 1.1 fusion.28
  382.2 1.3 multiply_reduce_fusion.1
  383.6 1.4 multiply_convert_fusion.1
  386.8 56.5 %all-gather.14.cloned.1.call-done = f32[256,1280]{1,0:T(8,128)} async-done(((f32[8,1280]{1,0:T(8,128)}), f32[256,1280]{1,0:T(8,128)}) %all-gather.14.cloned.1.call-update) | async-done | bytes 1310736 | tf_op jit(solution)/shard_map/all_gather | solution.py:133
  443.3 1.4 bitcast_reduce_fusion
  444.7 2.3 fusion.20
  447.5 76.1 %pmax.7 = f32[64]{0:T(128)S(1)} all-reduce(f32[64]{0:T(128)S(1)} %pad_maximum_fusion.1), channel_id=1, replica_groups=mesh['dp'=8,'tensor'=32] {'dp','tensor'}, use_global_device_ids=true, to_apply=%region_17.18 | all-reduce | flops 64 | bytes 512 | tf_op jit(solution)/shard_map/pmax | solution.py:151
  (85 shorter events, 9.4 us)
Async XLA Ops:
  7.2 267.7 %copy-start = (bf16[640,1280]{1,0:T(8,128)(2,1)S(1)}, bf16[640,1280]{1,0:T(8,128)(2,1)}, u32[]{:S(2)}) copy-start(bf16[640,1280]{1,0:T(8,128)(2,1)} %param.28) | copy-start | bytes 4915204
  7.2 87.7 %all-gather.10.cloned.1.call-start = ((), (), s32[]{:S(2)}) async-start(), calls=%async_computation.3 | async-start | bytes 11489280 | tf_op jit(solution)/shard_map/all_gather | solution.py:63
  8.5 3.5 copy-start.8
  11.9 3.4 copy-start.9
  14.0 3.2 copy-start.10
  17.1 169.9 %all-gather.12.cloned.1.call-start = ((), (), s32[]{:S(2)}) async-start(), calls=%async_computation.4 | async-start | bytes 2967552 | tf_op jit(solution)/shard_map/all_gather | solution.py:68
  105.5 163.9 %all-gather.8.cloned.1.call-start = ((), (), s32[]{:S(2)}) async-start(), calls=%async_computation.1 | async-start | bytes 2949120 | tf_op jit(solution)/shard_map/all_gather | solution.py:108
  106.3 14.1 %copy-start.5 = (pred[128,4096]{1,0:T(8,128)(4,1)}, pred[128,4096]{1,0:T(8,128)(4,1)S(1)}, u32[]{:S(2)}) copy-start(pred[128,4096]{1,0:T(8,128)(4,1)S(1)} %fusion.12) | copy-start | bytes 1572868
  141.7 25.4 %copy-start.4 = (bf16[640,1280]{1,0:T(8,128)(2,1)S(1)}, bf16[640,1280]{1,0:T(8,128)(2,1)}, u32[]{:S(2)}) copy-start(bf16[640,1280]{1,0:T(8,128)(2,1)} %param.22) | copy-start | bytes 4915204
  141.7 25.9 %copy-start.6 = (f32[1280]{0:T(1024)S(1)}, f32[1280]{0:T(1024)}, u32[]{:S(2)}) copy-start(f32[1280]{0:T(1024)} %param.23) | copy-start | bytes 15364
  167.1 1.0 copy-start.1
  167.6 101.8 %copy-start.11 = (bf16[1280,640]{1,0:T(8,128)(2,1)S(1)}, bf16[1280,640]{1,0:T(8,128)(2,1)}, u32[]{:S(2)}) copy-start(bf16[1280,640]{1,0:T(8,128)(2,1)} %param.24) | copy-start | bytes 4915204
  187.0 87.8 %copy-start.12 = (f32[640]{0:T(1024)S(1)}, f32[640]{0:T(1024)}, u32[]{:S(2)}) copy-start(f32[640]{0:T(1024)} %param.27) | copy-start | bytes 7684
  187.0 87.8 %copy-start.13 = (f32[640]{0:T(1024)S(1)}, f32[640]{0:T(1024)}, u32[]{:S(2)}) copy-start(f32[640]{0:T(1024)} %param.26) | copy-start | bytes 7684
  187.1 194.0 %reduce-scatter.2.cloned.1.call-start = ((), (), s32[]{:S(2)}) async-start(), calls=%async_computation.2 | async-start | bytes 2949120 | tf_op jit(solution)/shard_map/reduce_scatter | solution.py:112
  283.8 98.5 %copy-start.2 = (bf16[128,1280]{1,0:T(8,128)(2,1)S(1)}, bf16[128,1280]{1,0:T(8,128)(2,1)}, u32[]{:S(2)}) copy-start(bf16[128,1280]{1,0:T(8,128)(2,1)} %multiply_convert_fusion.2) | copy-start | bytes 983044
  283.8 98.5 %copy-start.7 = (f32[1280]{0:T(1024)S(1)}, f32[1280]{0:T(1024)}, u32[]{:S(2)}) copy-start(f32[1280]{0:T(1024)} %param.29) | copy-start | bytes 15364
  283.8 159.5 %all-gather.14.cloned.1.call-start = ((), (), s32[]{:S(2)}) async-start(), calls=%async_computation.5 | async-start | bytes 1351680 | tf_op jit(solution)/shard_map/all_gather | solution.py:133
  384.9 140.0 %copy-start.3 = (bf16[128,1280]{1,0:T(8,128)(2,1)}, bf16[128,1280]{1,0:T(8,128)(2,1)S(1)}, u32[]{:S(2)}) copy-start(bf16[128,1280]{1,0:T(8,128)(2,1)S(1)} %multiply_convert_fusion.1) | copy-start | bytes 983044
  384.9 138.6 %copy-start.14 = (s32[32]{0:T(128)S(1)}, s32[32]{0:T(128)}, u32[]{:S(2)}) copy-start(s32[32]{0:T(128)} %param.19) | copy-start | bytes 388
Sparse Core Ops, SparseCore 0:
  17.3 77.5 all-gather.9
  105.6 81.3 all-gather.11
  190.2 79.1 all-gather.7
  283.9 97.1 reduce-scatter.1
  386.1 57.0 all-gather.13

commit v5 on v4

--- a/solution.py
+++ b/solution.py
@@ -130,7 +130,12 @@
     row_sums = jnp.dot(member.T, result_f32, precision=lax.Precision.HIGHEST)
     last_rows = jnp.dot(chosen.T, result_f32, precision=lax.Precision.HIGHEST)
     partial = jnp.concatenate([row_sums, last_rows], axis=0)
-    summed = jnp.sum(lax.all_gather(partial, "tensor", axis=0, tiled=False), axis=0)
+    summed = jnp.sum(
+        lax.all_gather(partial.astype(jnp.bfloat16), "tensor", axis=0, tiled=False).astype(
+            jnp.float32
+        ),
+        axis=0,
+    )
     row_sums, last_rows = summed[:REQS], summed[REQS:]
     counts = tally.astype(jnp.float32)
     request_mean = row_sums / counts[:, None]

time: 532 us -> 515 us (0.968)
  waiting for transfers between devices: 328 us -> 274 us
  blocking collectives: 76.1 us -> 119 us
    all_gather x1 -> x0, waiting for transfers between devices: 56.5 us -> none  [local(): lax.all_gather(partial, 'tensor', axis=0, tiled=False)]
    all_gather x0 -> x1, blocking collectives: none -> 45.7 us  [local(): lax.all_gather(partial.astype(jnp.bfloat16), 'tensor', axis=0, tiled=False)]
  transfers between devices with their start and end apart: 5 -> 4, of which waited for: 5 -> 4; matrix products, arithmetic and copies ran while one was open for 13% -> 13% of each run, Pallas kernels for 0% -> 0%
where the time goes in v5:
time: 515 us; the launch traced here: 514 us
  waiting for transfers between devices  274 us (53%)
  blocking collectives  119 us (23%)
  matrix products  57.6 us (11%)
  other arithmetic  33.7 us (7%)
  local copies, waits for them, and re-layouts  15.4 us (3%)
  between operations  14.1 us (3%)
    reduce_scatter x1, waiting for transfers between devices, local(): lax.psum_scatter(jnp.dot(hidden, w_down, preferred_element_type=jnp.float...  96.2 us
    all_gather x1, waiting for transfers between devices, local(): received = lax.all_gather(mid_rows, 'dp', axis=0, tiled=True)  82.3 us
    all_gather x1, waiting for transfers between devices, local(): gathered = lax.all_gather(packed, 'tensor', axis=0, tiled=False)  74.5 us
    pmax x1, blocking collectives, local(): lax.pmax(jnp.concatenate([spread_max, spread_norm]), ('dp', 'tensor'))  73 us
    all_gather x1, blocking collectives, local(): lax.all_gather(partial.astype(jnp.bfloat16), 'tensor', axis=0, tiled=False)  45.7 us
    sub x1, other arithmetic, local(): scores - row_max[:, :, None]  21.3 us
    all_gather x1, waiting for transfers between devices, local(): vocab_all = lax.all_gather(vocab_pack, 'dp', axis=0, tiled=False)  21.2 us
    dot_general x1, matrix products, local(): jnp.dot(weights.astype(jnp.bfloat16).reshape(HEADS * row_count, total_key...  21 us
  transfers between devices with their start and end apart: 4, of which 4 were waited for; matrix products, arithmetic and copies ran while one was open for 13% of the time, Pallas kernels for 0%

profile of v5, /device:TPU:1, one launch (start us, length us, event | category | flops | bytes accessed | tf_op | source)
XLA Modules:
  0.0 514.0 jit_solution(17221994798950864421)
XLA Ops:
  7.2 1.2 fusion.31
  8.5 3.4 fusion.65
  12.0 0.9 copy.28
  12.9 1.0 reduce_sum.119
  14.0 0.9 copy.29
  15.3 1.0 multiply_convert_fusion.3
  17.2 3.2 concatenate.29
  20.4 74.5 %all-gather.8.cloned.1.call-done = bf16[4352,1280]{1,0:T(8,128)(2,1)} async-done(((bf16[136,1280]{1,0:T(8,128)(2,1)}), bf16[4352,1280]{1,0:T(8,128)(2,1)}) %all-gather.8.cloned.1.call-update) | async-done | bytes 11141136 | tf_op jit(solution)/shard_map/all_gather | solution.py:63
  95.7 9.8 %fusion.67 = (bf16[32,128,640]{2,1,0:T(8,128)(2,1)}, bf16[32,128,640]{2,1,0:T(8,128)(2,1)}) fusion(bf16[32,136,1280]{2,1,0:T(8,128)(2,1)} %bitcast.59), kind=kLoop, calls=%fused_computation.116 | loop fusion | bytes 20971520 | tf_op jit(solution)/shard_map/slice | solution.py:69
  106.3 13.9 %fusion.17 = f32[10,128,4096]{2,1,0:T(8,128)} fusion(bf16[4096,640,1]{1,0,2:T(8,128)(2,1)} %bitcast.61, bf16[10,640]{1,0:T(8,128)(2,1)S(1)} %get-tuple-element.29, bf16[128,640]{1,0:T(8,128)(2,1)S(1)} %get-tuple-element.25), kind=kOutput, calls=%fused_computation.21 | convolution fusion | flops 6711705600 | bytes 26391040 | tf_op jit(solution)/shard_map/dot_general | solution.py:84
  120.2 21.3 %fusion.68 = f32[10,128]{1,0:T(8,128)S(1)} fusion(f32[10,128,4096]{2,1,0:T(8,128)} %fusion.17, pred[128,4096]{1,0:T(8,128)(4,1)S(1)} %fusion.14), kind=kOutput, calls=%fused_computation.117 | output fusion | flops 31461376 | bytes 21500928 | tf_op jit(solution)/shard_map/sub | solution.py:94
  141.5 21.0 %multiply_reduce_fusion = bf16[128,640]{1,0:T(8,128)(2,1)S(1)} fusion(bf16[4096,640,1]{1,0,2:T(8,128)(2,1)} %bitcast.60, f32[10,640]{1,0:T(8,128)S(1)} %get-tuple-element.30, f32[10,128]{1,0:T(8,128)S(1)} %fusion.68, f32[10,128,4096]{2,1,0:T(8,128)} %fusion.17, pred[128,4096]{1,0:T(8,128)(4,1)S(1)} %fusion.14), kind=kOutput, calls=%fused_computation.11 | convolution fusion | flops 6744724480 | bytes 26933248 | tf_op jit(solution)/shard_map/dot_general | solution.py:96
  162.6 2.0 multiply_reduce_fusion.3
  164.9 1.0 multiply_convert_fusion.2
  165.9 21.2 %all-gather.10.cloned.1.call-done = bf16[10304,125]{1,0:T(8,128)(2,1)} async-done(((bf16[1288,125]{1,0:T(8,128)(2,1)}), bf16[10304,125]{1,0:T(8,128)(2,1)}) %all-gather.10.cloned.1.call-update) | async-done | bytes 2576016 | tf_op jit(solution)/shard_map/all_gather | solution.py:68
  187.1 82.3 %all-gather.6.cloned.1.call-done = bf16[1024,1280]{1,0:T(8,128)(2,1)} async-done(((bf16[128,1280]{1,0:T(8,128)(2,1)}), bf16[1024,1280]{1,0:T(8,128)(2,1)}) %all-gather.6.cloned.1.call-update) | async-done | bytes 2621456 | tf_op jit(solution)/shard_map/all_gather | solution.py:108
  269.4 5.9 %fusion.69 = f32[1024,640]{1,0:T(8,128)} fusion(bf16[1024,1280]{1,0:T(8,128)(2,1)} %all-gather.6.cloned.1.call-done, bf16[1280,640]{1,0:T(8,128)(2,1)} %param.24), kind=kOutput, calls=%fused_computation.118 | convolution fusion | flops 1677721600 | bytes 6881280 | tf_op jit(solution)/shard_map/dot_general | solution.py:109
  275.4 9.0 %convolution_convert_fusion = bf16[1024,1280]{1,0:T(8,128)(2,1)} fusion(bf16[640,1280]{1,0:T(8,128)(2,1)S(1)} %copy-done, f32[1024,640]{1,0:T(8,128)} %fusion.69, bf16[1024,1280]{1,0:T(8,128)(2,1)} %all-gather.6.cloned.1.call-done, bf16[1280,640]{1,0:T(8,128)(2,1)} %param.25, f32[640]{0:T(1024)S(1)} %copy-done.10, f32[640]{0:T(1024)S(1)} %copy-done.11), kind=kOutput, calls=%fused_computation.10 | convolution fusion | flops 3361996800 | bytes 11146240 | tf_op jit(solution)/shard_map/dot_general | solution.py:113
  285.5 96.2 %reduce-scatter.2.cloned.1.call-done = bf16[128,1280]{1,0:T(8,128)(2,1)} async-done(((bf16[1024,1280]{1,0:T(8,128)(2,1)}), bf16[128,1280]{1,0:T(8,128)(2,1)}) %reduce-scatter.2.cloned.1.call-update) | async-done | bytes 327696 | tf_op jit(solution)/shard_map/reduce_scatter | solution.py:112
  381.7 1.3 fusion.30
  383.0 1.3 multiply_reduce_fusion.1
  384.3 1.4 multiply_convert_fusion.1
  386.2 45.7 %all_gather.24 = bf16[32,8,1280]{2,1,0:T(8,128)(2,1)S(1)} all-gather(bf16[1,8,1280]{2,1,0:T(8,128)(2,1)S(1)} %pad_maximum_fusion), channel_id=1, replica_groups=mesh['dp'=8,'tensor'=32] {'tensor'}, dimensions={0}, use_global_device_ids=true | all-gather | bytes 675840 | tf_op jit(solution)/shard_map/all_gather | solution.py:134
  433.0 73.0 %pmax.7 = f32[64]{0:T(128)S(1)} all-reduce(f32[64]{0:T(128)S(1)} %pad_maximum_fusion.1), channel_id=1, replica_groups=mesh['dp'=8,'tensor'=32] {'dp','tensor'}, use_global_device_ids=true, to_apply=%region_17.18 | all-reduce | flops 64 | bytes 512 | tf_op jit(solution)/shard_map/pmax | solution.py:156
  (79 shorter events, 7.6 us)
Async XLA Ops:
  7.2 268.2 %copy-start = (bf16[640,1280]{1,0:T(8,128)(2,1)S(1)}, bf16[640,1280]{1,0:T(8,128)(2,1)}, u32[]{:S(2)}) copy-start(bf16[640,1280]{1,0:T(8,128)(2,1)} %param.28) | copy-start | bytes 4915204
  7.2 87.7 %all-gather.8.cloned.1.call-start = ((), (), s32[]{:S(2)}) async-start(), calls=%async_computation.3 | async-start | bytes 11489280 | tf_op jit(solution)/shard_map/all_gather | solution.py:63
  8.5 3.5 copy-start.7
  11.9 3.4 copy-start.8
  12.0 5.2 %copy-start.9 = (bf16[125]{0:T(256)(128)(2,1)S(1)}, bf16[125]{0:T(256)(128)(2,1)}, u32[]{:S(2)}) copy-start(bf16[125]{0:T(256)(128)(2,1)} %param.31) | copy-start | bytes 754
  17.1 169.9 %all-gather.10.cloned.1.call-start = ((), (), s32[]{:S(2)}) async-start(), calls=%async_computation.4 | async-start | bytes 2967552 | tf_op jit(solution)/shard_map/all_gather | solution.py:68
  105.5 163.9 %all-gather.6.cloned.1.call-start = ((), (), s32[]{:S(2)}) async-start(), calls=%async_computation.1 | async-start | bytes 2949120 | tf_op jit(solution)/shard_map/all_gather | solution.py:108
  141.5 23.0 %copy-start.1 = (bf16[1,128,1280]{2,1,0:T(8,128)(2,1)S(1)}, bf16[1,128,1280]{2,1,0:T(8,128)(2,1)}, u32[]{:S(2)}) copy-start(bf16[1,128,1280]{2,1,0:T(8,128)(2,1)} %param.17) | copy-start | bytes 983044
  141.5 23.0 %copy-start.5 = (f32[1280]{0:T(1024)S(1)}, f32[1280]{0:T(1024)}, u32[]{:S(2)}) copy-start(f32[1280]{0:T(1024)} %param.23) | copy-start | bytes 15364
  187.1 88.3 %copy-start.10 = (f32[640]{0:T(1024)S(1)}, f32[640]{0:T(1024)}, u32[]{:S(2)}) copy-start(f32[640]{0:T(1024)} %param.27) | copy-start | bytes 7684
  187.1 88.3 %copy-start.11 = (f32[640]{0:T(1024)S(1)}, f32[640]{0:T(1024)}, u32[]{:S(2)}) copy-start(f32[640]{0:T(1024)} %param.26) | copy-start | bytes 7684
  187.1 194.6 %reduce-scatter.2.cloned.1.call-start = ((), (), s32[]{:S(2)}) async-start(), calls=%async_computation.2 | async-start | bytes 2949120 | tf_op jit(solution)/shard_map/reduce_scatter | solution.py:112
  275.3 107.7 %copy-start.2 = (bf16[128,1280]{1,0:T(8,128)(2,1)S(1)}, bf16[128,1280]{1,0:T(8,128)(2,1)}, u32[]{:S(2)}) copy-start(bf16[128,1280]{1,0:T(8,128)(2,1)} %multiply_convert_fusion.2) | copy-start | bytes 983044
  275.4 107.7 %copy-start.6 = (f32[1280]{0:T(1024)S(1)}, f32[1280]{0:T(1024)}, u32[]{:S(2)}) copy-start(f32[1280]{0:T(1024)} %param.29) | copy-start | bytes 15364
  381.7 50.3 %copy-start.4 = (bf16[10304,125]{1,0:T(8,128)(2,1)S(1)}, bf16[10304,125]{1,0:T(8,128)(2,1)}, u32[]{:S(2)}) copy-start(bf16[10304,125]{1,0:T(8,128)(2,1)} %all-gather.10.cloned.1.call-done) | copy-start | bytes 7728004
  383.0 123.0 %copy-start.12 = (s32[32]{0:T(128)S(1)}, s32[32]{0:T(128)}, u32[]{:S(2)}) copy-start(s32[32]{0:T(128)} %param.19) | copy-start | bytes 388
  385.7 121.7 %copy-start.3 = (bf16[128,1280]{1,0:T(8,128)(2,1)}, bf16[128,1280]{1,0:T(8,128)(2,1)S(1)}, u32[]{:S(2)}) copy-start(bf16[128,1280]{1,0:T(8,128)(2,1)S(1)} %multiply_convert_fusion.1) | copy-start | bytes 983044
Sparse Core Ops, SparseCore 0:
  17.3 77.5 all-gather.7
  105.6 81.3 all-gather.9
  190.2 79.1 all-gather.5
  284.5 97.2 reduce-scatter.1

commit v6 on v5

--- a/solution.py
+++ b/solution.py
@@ -64,8 +64,14 @@
     vocab_pack = jnp.concatenate(
         [w_vocab, logit_gain[None], jnp.zeros((7, w_vocab.shape[1]), w_vocab.dtype)], axis=0
     )
-    vocab_pack, gathered = lax.optimization_barrier((vocab_pack, gathered))
-    vocab_all = lax.all_gather(vocab_pack, "dp", axis=0, tiled=False)
+    dp_size = lax.axis_size("dp")
+    vocab_all = jnp.stack(
+        [vocab_pack]
+        + [
+            lax.ppermute(vocab_pack, "dp", [(i, (i + shift) % dp_size) for i in range(dp_size)])
+            for shift in range(1, dp_size)
+        ]
+    )
     key_all = gathered[:, :row_count, :head_width].reshape(-1, head_width)
     value_all = gathered[:, :row_count, head_width:].reshape(-1, head_width)
     seg_all = gathered[:, row_count, :row_count].reshape(-1).astype(jnp.int32)

time: 515 us -> 549 us (1.066)
  starting transfers between devices: 0.34 us -> 24.8 us
  local copies, waits for them, and re-layouts: 15.4 us -> 21.8 us
    ppermute x0 -> x7, waiting for transfers between devices: none -> 66.2 us  [local(): lax.ppermute(vocab_pack, 'dp', [(i, (i + shift) % dp_size) for i in range...]
    all_gather x1, waiting for transfers between devices: 74.5 us -> 34 us  [local(): gathered = lax.all_gather(packed, 'tensor', axis=0, tiled=False)]
    ppermute x0 -> x7, starting transfers between devices: none -> 24.7 us  [local(): lax.ppermute(vocab_pack, 'dp', [(i, (i + shift) % dp_size) for i in range...]
    all_gather x1 -> x0, waiting for transfers between devices: 21.2 us -> none  [local(): vocab_all = lax.all_gather(vocab_pack, 'dp', axis=0, tiled=False)]
    unnamed x26 -> x39, local copies, waits for them, and re-layouts: 0.08 us -> 6.75 us
    all_gather x1, waiting for transfers between devices: 82.3 us -> 76.1 us  [local(): received = lax.all_gather(mid_rows, 'dp', axis=0, tiled=True)]
  transfers between devices with their start and end apart: 4 -> 10, of which waited for: 4 -> 6; matrix products, arithmetic and copies ran while one was open for 13% -> 2% of each run, Pallas kernels for 0% -> 0%
where the time goes in v6:
time: 549 us; the launch traced here: 548 us
  waiting for transfers between devices  273 us (50%)
  blocking collectives  119 us (22%)
  matrix products  61.9 us (11%)
  other arithmetic  34.2 us (6%)
  starting transfers between devices  24.8 us (5%)
  local copies, waits for them, and re-layouts  21.8 us (4%)
  between operations  14.1 us (3%)
    reduce_scatter x1, waiting for transfers between devices, local(): lax.psum_scatter(jnp.dot(hidden, w_down, preferred_element_type=jnp.float...  96.3 us
    all_gather x1, waiting for transfers between devices, local(): received = lax.all_gather(mid_rows, 'dp', axis=0, tiled=True)  76.1 us
    pmax x1, blocking collectives, local(): lax.pmax(jnp.concatenate([spread_max, spread_norm]), ('dp', 'tensor'))  73 us
    ppermute x7, waiting for transfers between devices, local(): lax.ppermute(vocab_pack, 'dp', [(i, (i + shift) % dp_size) for i in range...  66.2 us
    all_gather x1, blocking collectives, local(): lax.all_gather(partial.astype(jnp.bfloat16), 'tensor', axis=0, tiled=False)  45.6 us
    all_gather x1, waiting for transfers between devices, local(): gathered = lax.all_gather(packed, 'tensor', axis=0, tiled=False)  34 us
    dot_general x1, matrix products, local(): jnp.dot(weights.astype(jnp.bfloat16).reshape(HEADS * row_count, total_key...  25.4 us
    ppermute x7, starting transfers between devices, local(): lax.ppermute(vocab_pack, 'dp', [(i, (i + shift) % dp_size) for i in range...  24.7 us
  transfers between devices with their start and end apart: 10, of which 6 were waited for; matrix products, arithmetic and copies ran while one was open for 2% of the time, Pallas kernels for 0%

profile of v6, /device:TPU:1, one launch (start us, length us, event | category | flops | bytes accessed | tf_op | source)
XLA Modules:
  0.0 548.0 jit_solution(17925992749069137036)
XLA Ops:
  8.5 3.4 fusion.65
  15.3 1.7 multiply_convert_fusion.3
  17.9 2.2 concatenate.31
  20.0 10.0 %collective-permute-start.6 = (bf16[1288,125]{1,0:T(8,128)(2,1)S(1)}, bf16[1288,125]{1,0:T(8,128)(2,1)S(1)}, u32[]{:S(2)}, u32[]{:S(2)}) collective-permute-start(bf16[1288,125]{1,0:T(8,128)(2,1)S(1)} %concatenate.31), channel_id=1, source_target_pairs={{0,224},{32,0},{64,32},{96,64},{128,96},{160,128},{192,160},{224,1... | collective-permute-start | bytes 966008 | tf_op jit(solution)/shard_map/ppermute | solution.py:71
  30.6 2.5 collective-permute-start.3
  33.1 5.3 collective-permute-start
  39.1 46.2 %collective-permute-done = bf16[1288,125]{1,0:T(8,128)(2,1)} collective-permute-done((bf16[1288,125]{1,0:T(8,128)(2,1)S(1)}, bf16[1288,125]{1,0:T(8,128)(2,1)}, u32[]{:S(2)}, u32[]{:S(2)}) %collective-permute-start) | collective-permute-done | bytes 322032 | tf_op jit(solution)/shard_map/ppermute | solution.py:71
  85.4 1.7 bitcast_dynamic-update-slice_fusion.6
  87.1 5.4 collective-permute-done.1
  92.5 6.3 %collective-permute-start.2 = (bf16[1288,125]{1,0:T(8,128)(2,1)S(1)}, bf16[1288,125]{1,0:T(8,128)(2,1)S(1)}, u32[]{:S(2)}, u32[]{:S(2)}) collective-permute-start(bf16[1288,125]{1,0:T(8,128)(2,1)S(1)} %concatenate.31), channel_id=1, source_target_pairs={{0,96},{32,128},{64,160},{96,192},{128,224},{160,0},{192,32},{224,... | collective-permute-start | bytes 966008 | tf_op jit(solution)/shard_map/ppermute | solution.py:71
  99.6 14.5 %collective-permute-done.2 = bf16[1288,125]{1,0:T(8,128)(2,1)S(1)} collective-permute-done((bf16[1288,125]{1,0:T(8,128)(2,1)S(1)}, bf16[1288,125]{1,0:T(8,128)(2,1)S(1)}, u32[]{:S(2)}, u32[]{:S(2)}) %collective-permute-start.2) | collective-permute-done | bytes 322032 | tf_op jit(solution)/shard_map/ppermute | solution.py:71
  117.9 34.0 %all-gather.6.cloned.1.call-done = bf16[4352,1280]{1,0:T(8,128)(2,1)} async-done(((bf16[136,1280]{1,0:T(8,128)(2,1)}), bf16[4352,1280]{1,0:T(8,128)(2,1)}) %all-gather.6.cloned.1.call-update) | async-done | bytes 11141136 | tf_op jit(solution)/shard_map/all_gather | solution.py:63
  152.8 9.8 %fusion.67 = (bf16[32,128,640]{2,1,0:T(8,128)(2,1)}, bf16[32,128,640]{2,1,0:T(8,128)(2,1)}) fusion(bf16[32,136,1280]{2,1,0:T(8,128)(2,1)} %bitcast.74), kind=kLoop, calls=%fused_computation.124 | loop fusion | bytes 20971520 | tf_op jit(solution)/shard_map/slice | solution.py:75
  163.1 14.1 %fusion.17 = f32[10,128,4096]{2,1,0:T(8,128)} fusion(bf16[4096,640,1]{1,0,2:T(8,128)(2,1)} %bitcast.76, bf16[10,640]{1,0:T(8,128)(2,1)S(1)} %get-tuple-element.25, bf16[128,640]{1,0:T(8,128)(2,1)S(1)} %copy-done.6), kind=kOutput, calls=%fused_computation.21 | convolution fusion | flops 6711705600 | bytes 26391040 | tf_op jit(solution)/shard_map/dot_general | solution.py:90
  177.2 21.3 %fusion.68 = f32[10,128]{1,0:T(8,128)S(1)} fusion(f32[10,128,4096]{2,1,0:T(8,128)} %fusion.17, pred[128,4096]{1,0:T(8,128)(4,1)S(1)} %fusion.14), kind=kOutput, calls=%fused_computation.125 | output fusion | flops 31461376 | bytes 21500928 | tf_op jit(solution)/shard_map/sub | solution.py:100
  198.6 25.4 %multiply_reduce_fusion = bf16[128,640]{1,0:T(8,128)(2,1)S(1)} fusion(bf16[4096,640,1]{1,0,2:T(8,128)(2,1)} %bitcast.75, f32[10,640]{1,0:T(8,128)S(1)} %get-tuple-element.26, f32[10,128]{1,0:T(8,128)S(1)} %fusion.68, f32[10,128,4096]{2,1,0:T(8,128)} %fusion.17, pred[128,4096]{1,0:T(8,128)(4,1)} %copy-done.5), kind=kOutput, calls=%fused_computation.11 | convolution fusion | flops 6744724480 | bytes 26933248 | tf_op jit(solution)/shard_map/dot_general | solution.py:102
  226.3 76.1 %all-gather.4.cloned.1.call-done = bf16[1024,1280]{1,0:T(8,128)(2,1)} async-done(((bf16[128,1280]{1,0:T(8,128)(2,1)}), bf16[1024,1280]{1,0:T(8,128)(2,1)}) %all-gather.4.cloned.1.call-update) | async-done | bytes 2621456 | tf_op jit(solution)/shard_map/all_gather | solution.py:114
  302.5 5.4 fusion.69
  307.9 8.9 %convolution_convert_fusion = bf16[1024,1280]{1,0:T(8,128)(2,1)} fusion(bf16[640,1280]{1,0:T(8,128)(2,1)S(1)} %copy-done, f32[1024,640]{1,0:T(8,128)} %fusion.69, bf16[1024,1280]{1,0:T(8,128)(2,1)} %all-gather.4.cloned.1.call-done, bf16[1280,640]{1,0:T(8,128)(2,1)} %param.25, f32[640]{0:T(1024)S(1)} %copy-done.13, f32[640]{0:T(1024)S(1)} %copy-done.14), kind=kOutput, calls=%fused_computation.10 | convolution fusion | flops 3361996800 | bytes 11146240 | tf_op jit(solution)/shard_map/dot_general | solution.py:119
  318.0 96.3 %reduce-scatter.2.cloned.1.call-done = bf16[128,1280]{1,0:T(8,128)(2,1)} async-done(((bf16[1024,1280]{1,0:T(8,128)(2,1)}), bf16[128,1280]{1,0:T(8,128)(2,1)}) %reduce-scatter.2.cloned.1.call-update) | async-done | bytes 327696 | tf_op jit(solution)/shard_map/reduce_scatter | solution.py:118
  416.8 1.4 multiply_convert_fusion.1
  418.6 45.6 %all_gather.16 = bf16[32,8,1280]{2,1,0:T(8,128)(2,1)S(1)} all-gather(bf16[1,8,1280]{2,1,0:T(8,128)(2,1)S(1)} %pad_maximum_fusion), channel_id=1, replica_groups=mesh['dp'=8,'tensor'=32] {'tensor'}, dimensions={0}, use_global_device_ids=true | all-gather | bytes 675840 | tf_op jit(solution)/shard_map/all_gather | solution.py:140
  464.3 2.3 fusion.22
  467.1 73.0 %pmax.7 = f32[64]{0:T(128)S(1)} all-reduce(f32[64]{0:T(128)S(1)} %pad_maximum_fusion.1), channel_id=1, replica_groups=mesh['dp'=8,'tensor'=32] {'dp','tensor'}, use_global_device_ids=true, to_apply=%region_17.18 | all-reduce | flops 64 | bytes 512 | tf_op jit(solution)/shard_map/pmax | solution.py:162
  (104 shorter events, 21.1 us)
Async XLA Ops:
  7.2 300.7 %copy-start = (bf16[640,1280]{1,0:T(8,128)(2,1)S(1)}, bf16[640,1280]{1,0:T(8,128)(2,1)}, u32[]{:S(2)}) copy-start(bf16[640,1280]{1,0:T(8,128)(2,1)} %param.28) | copy-start | bytes 4915204
  7.2 144.7 %all-gather.6.cloned.1.call-start = ((), (), s32[]{:S(2)}) async-start(), calls=%async_computation.3 | async-start | bytes 11489280 | tf_op jit(solution)/shard_map/all_gather | solution.py:63
  8.5 3.5 copy-start.9
  14.0 3.9 copy-start.11
  17.8 284.7 %all-gather.4.cloned.1.call-start = ((), (), s32[]{:S(2)}) async-start(), calls=%async_computation.1 | async-start | bytes 2949120 | tf_op jit(solution)/shard_map/all_gather | solution.py:114
  20.0 97.1 %collective-permute-start.6 = (bf16[1288,125]{1,0:T(8,128)(2,1)S(1)}, bf16[1288,125]{1,0:T(8,128)(2,1)S(1)}, u32[]{:S(2)}, u32[]{:S(2)}) collective-permute-start(bf16[1288,125]{1,0:T(8,128)(2,1)S(1)} %concatenate.31), channel_id=1, source_target_pairs={{0,224},{32,0},{64,32},{96,64},{128,96},{160,128},{192,160},{224,1... | collective-permute-start | bytes 966008 | tf_op jit(solution)/shard_map/ppermute | solution.py:71
  30.0 86.4 %collective-permute-start.5 = (bf16[1288,125]{1,0:T(8,128)(2,1)S(1)}, bf16[1288,125]{1,0:T(8,128)(2,1)S(1)}, u32[]{:S(2)}, u32[]{:S(2)}) collective-permute-start(bf16[1288,125]{1,0:T(8,128)(2,1)S(1)} %concatenate.31), channel_id=1, source_target_pairs={{0,192},{32,224},{64,0},{96,32},{128,64},{160,96},{192,128},{224,1... | collective-permute-start | bytes 966008 | tf_op jit(solution)/shard_map/ppermute | solution.py:71
  30.6 85.1 %collective-permute-start.4 = (bf16[1288,125]{1,0:T(8,128)(2,1)S(1)}, bf16[1288,125]{1,0:T(8,128)(2,1)S(1)}, u32[]{:S(2)}, u32[]{:S(2)}) collective-permute-start(bf16[1288,125]{1,0:T(8,128)(2,1)S(1)} %concatenate.31), channel_id=1, source_target_pairs={{0,160},{32,192},{64,224},{96,0},{128,32},{160,64},{192,96},{224,1... | collective-permute-start | bytes 966008 | tf_op jit(solution)/shard_map/ppermute | solution.py:71
  30.6 84.2 %collective-permute-start.3 = (bf16[1288,125]{1,0:T(8,128)(2,1)S(1)}, bf16[1288,125]{1,0:T(8,128)(2,1)S(1)}, u32[]{:S(2)}, u32[]{:S(2)}) collective-permute-start(bf16[1288,125]{1,0:T(8,128)(2,1)S(1)} %concatenate.31), channel_id=1, source_target_pairs={{0,128},{32,160},{64,192},{96,224},{128,0},{160,32},{192,64},{224,... | collective-permute-start | bytes 966008 | tf_op jit(solution)/shard_map/ppermute | solution.py:71
  33.1 52.3 %collective-permute-start = (bf16[1288,125]{1,0:T(8,128)(2,1)S(1)}, bf16[1288,125]{1,0:T(8,128)(2,1)}, u32[]{:S(2)}, u32[]{:S(2)}) collective-permute-start(bf16[1288,125]{1,0:T(8,128)(2,1)S(1)} %concatenate.31), channel_id=1, source_target_pairs={{0,32},{32,64},{64,96},{96,128},{128,160},{160,192},{192,224},{224... | collective-permute-start | bytes 966008 | tf_op jit(solution)/shard_map/ppermute | solution.py:71
  85.4 7.2 %collective-permute-start.1 = (bf16[1288,125]{1,0:T(8,128)(2,1)S(1)}, bf16[1288,125]{1,0:T(8,128)(2,1)S(1)}, u32[]{:S(2)}, u32[]{:S(2)}) collective-permute-start(bf16[1288,125]{1,0:T(8,128)(2,1)S(1)} %concatenate.31), channel_id=1, source_target_pairs={{0,64},{32,96},{64,128},{96,160},{128,192},{160,224},{192,0},{224,... | collective-permute-start | bytes 966008 | tf_op jit(solution)/shard_map/ppermute | solution.py:71
  92.5 21.6 %collective-permute-start.2 = (bf16[1288,125]{1,0:T(8,128)(2,1)S(1)}, bf16[1288,125]{1,0:T(8,128)(2,1)S(1)}, u32[]{:S(2)}, u32[]{:S(2)}) collective-permute-start(bf16[1288,125]{1,0:T(8,128)(2,1)S(1)} %concatenate.31), channel_id=1, source_target_pairs={{0,96},{32,128},{64,160},{96,192},{128,224},{160,0},{192,32},{224,... | collective-permute-start | bytes 966008 | tf_op jit(solution)/shard_map/ppermute | solution.py:71
  152.8 10.3 %copy-start.6 = (bf16[128,640]{1,0:T(8,128)(2,1)S(1)}, bf16[128,640]{1,0:T(8,128)(2,1)}, u32[]{:S(2)}) copy-start(bf16[128,640]{1,0:T(8,128)(2,1)} %get-tuple-element.21) | copy-start | bytes 491524
  163.1 14.1 %copy-start.5 = (pred[128,4096]{1,0:T(8,128)(4,1)}, pred[128,4096]{1,0:T(8,128)(4,1)S(1)}, u32[]{:S(2)}) copy-start(pred[128,4096]{1,0:T(8,128)(4,1)S(1)} %fusion.14) | copy-start | bytes 1572868
  198.5 25.4 %copy-start.4 = (bf16[640,1280]{1,0:T(8,128)(2,1)S(1)}, bf16[640,1280]{1,0:T(8,128)(2,1)}, u32[]{:S(2)}) copy-start(bf16[640,1280]{1,0:T(8,128)(2,1)} %param.22) | copy-start | bytes 4915204
  198.5 25.9 %copy-start.7 = (f32[1280]{0:T(1024)S(1)}, f32[1280]{0:T(1024)}, u32[]{:S(2)}) copy-start(f32[1280]{0:T(1024)} %param.23) | copy-start | bytes 15364
  224.5 78.0 %copy-start.12 = (bf16[1280,640]{1,0:T(8,128)(2,1)S(1)}, bf16[1280,640]{1,0:T(8,128)(2,1)}, u32[]{:S(2)}) copy-start(bf16[1280,640]{1,0:T(8,128)(2,1)} %param.24) | copy-start | bytes 4915204
  226.2 81.7 %copy-start.13 = (f32[640]{0:T(1024)S(1)}, f32[640]{0:T(1024)}, u32[]{:S(2)}) copy-start(f32[640]{0:T(1024)} %param.27) | copy-start | bytes 7684
  226.3 81.7 %copy-start.14 = (f32[640]{0:T(1024)S(1)}, f32[640]{0:T(1024)}, u32[]{:S(2)}) copy-start(f32[640]{0:T(1024)} %param.26) | copy-start | bytes 7684
  226.3 188.0 %reduce-scatter.2.cloned.1.call-start = ((), (), s32[]{:S(2)}) async-start(), calls=%async_computation.2 | async-start | bytes 2949120 | tf_op jit(solution)/shard_map/reduce_scatter | solution.py:118
  316.8 98.6 %copy-start.2 = (bf16[128,1280]{1,0:T(8,128)(2,1)S(1)}, bf16[128,1280]{1,0:T(8,128)(2,1)}, u32[]{:S(2)}) copy-start(bf16[128,1280]{1,0:T(8,128)(2,1)} %multiply_convert_fusion.2) | copy-start | bytes 983044
  316.8 98.6 %copy-start.8 = (f32[1280]{0:T(1024)S(1)}, f32[1280]{0:T(1024)}, u32[]{:S(2)}) copy-start(f32[1280]{0:T(1024)} %param.29) | copy-start | bytes 15364
  418.1 123.4 %copy-start.3 = (bf16[128,1280]{1,0:T(8,128)(2,1)}, bf16[128,1280]{1,0:T(8,128)(2,1)S(1)}, u32[]{:S(2)}) copy-start(bf16[128,1280]{1,0:T(8,128)(2,1)S(1)} %multiply_convert_fusion.1) | copy-start | bytes 983044
  418.1 121.9 %copy-start.15 = (s32[32]{0:T(128)S(1)}, s32[32]{0:T(128)}, u32[]{:S(2)}) copy-start(s32[32]{0:T(128)} %param.19) | copy-start | bytes 388
  (2 other events, 4.3 us)
Sparse Core Ops, SparseCore 0:
  17.9 133.9 all-gather.5
  226.4 76.0 all-gather.3
  317.0 97.2 reduce-scatter.1

commit v7 on v5

--- a/solution.py
+++ b/solution.py
@@ -54,12 +54,7 @@
     )
     value_rows = projected[:, 2 * head_width :].astype(jnp.bfloat16)
     score_scale = 1.0 / math.sqrt(HD)
-    seg_block = jnp.zeros((8, 2 * head_width), jnp.bfloat16).at[0, :row_count].set(
-        segments.astype(jnp.bfloat16)
-    )
-    packed = jnp.concatenate(
-        [jnp.concatenate([key_rows, value_rows], axis=1), seg_block], axis=0
-    )
+    packed = jnp.concatenate([key_rows, value_rows], axis=1)
     gathered = lax.all_gather(packed, "tensor", axis=0, tiled=False)
     vocab_pack = jnp.concatenate(
         [w_vocab, logit_gain[None], jnp.zeros((7, w_vocab.shape[1]), w_vocab.dtype)], axis=0
@@ -68,7 +63,7 @@
     vocab_all = lax.all_gather(vocab_pack, "dp", axis=0, tiled=False)
     key_all = gathered[:, :row_count, :head_width].reshape(-1, head_width)
     value_all = gathered[:, :row_count, head_width:].reshape(-1, head_width)
-    seg_all = gathered[:, row_count, :row_count].reshape(-1).astype(jnp.int32)
+    seg_all = lax.all_gather(segments, "tensor", axis=0, tiled=True)
     tally = jnp.sum((seg_all[:, None] == request_numbers[None, :]).astype(jnp.int32), axis=0)
     total_keys = key_all.shape[0]
     key_pos = jnp.arange(total_keys, dtype=jnp.int32)

time: 515 us -> 513 us (level)
  waiting for transfers between devices: 274 us -> 223 us
  blocking collectives: 119 us -> 165 us
    all_gather x1, waiting for transfers between devices: 74.5 us -> 26.5 us  [local(): gathered = lax.all_gather(packed, 'tensor', axis=0, tiled=False)]
    all_gather x0 -> x1, blocking collectives: none -> 46.1 us  [local(): seg_all = lax.all_gather(segments, 'tensor', axis=0, tiled=True)]
where the time goes in v7:
time: 513 us; the launch traced here: 512 us
  waiting for transfers between devices  223 us (43%)
  blocking collectives  165 us (32%)
  matrix products  61.7 us (12%)
  other arithmetic  32.6 us (6%)
  local copies, waits for them, and re-layouts  15.6 us (3%)
  between operations  14.1 us (3%)
    reduce_scatter x1, waiting for transfers between devices, local(): lax.psum_scatter(jnp.dot(hidden, w_down, preferred_element_type=jnp.float...  95.8 us
    all_gather x1, waiting for transfers between devices, local(): received = lax.all_gather(mid_rows, 'dp', axis=0, tiled=True)  82.3 us
    pmax x1, blocking collectives, local(): lax.pmax(jnp.concatenate([spread_max, spread_norm]), ('dp', 'tensor'))  73 us
    all_gather x1, blocking collectives, local(): seg_all = lax.all_gather(segments, 'tensor', axis=0, tiled=True)  46.1 us
    all_gather x1, blocking collectives, local(): lax.all_gather(partial.astype(jnp.bfloat16), 'tensor', axis=0, tiled=False)  45.7 us
    all_gather x1, waiting for transfers between devices, local(): gathered = lax.all_gather(packed, 'tensor', axis=0, tiled=False)  26.5 us
    dot_general x1, matrix products, local(): jnp.dot(weights.astype(jnp.bfloat16).reshape(HEADS * row_count, total_key...  25.4 us
    sub x1, other arithmetic, local(): scores - row_max[:, :, None]  21.3 us
  transfers between devices with their start and end apart: 4, of which 4 were waited for; matrix products, arithmetic and copies ran while one was open for 13% of the time, Pallas kernels for 0%

profile of v7, /device:TPU:1, one launch (start us, length us, event | category | flops | bytes accessed | tf_op | source)
XLA Modules:
  0.0 512.2 jit_solution(11117079274914719107)
XLA Ops:
  7.2 1.2 fusion.30
  8.5 3.4 fusion.63
  12.0 0.9 copy.26
  12.9 1.0 reduce_sum.118
  15.3 1.0 multiply_convert_fusion.4
  17.2 3.1 concatenate.24
  20.3 46.1 %all-gather = s32[1,4096]{1,0:T(1,128)S(1)} all-gather(s32[1,128]{1,0:T(1,128)S(1)} %copy-done.8), channel_id=2, replica_groups=mesh['dp'=8,'tensor'=32] {'tensor'}, dimensions={1}, use_global_device_ids=true | all-gather | bytes 16896 | tf_op jit(solution)/shard_map/all_gather | solution.py:66
  66.9 26.5 %all-gather.9.cloned.1.call-done = bf16[4096,1280]{1,0:T(8,128)(2,1)} async-done(((bf16[128,1280]{1,0:T(8,128)(2,1)}), bf16[4096,1280]{1,0:T(8,128)(2,1)}) %all-gather.9.cloned.1.call-update) | async-done | bytes 10485776 | tf_op jit(solution)/shard_map/all_gather | solution.py:58
  93.5 9.6 %fusion.65 = (bf16[32,128,640]{2,1,0:T(8,128)(2,1)}, bf16[32,128,640]{2,1,0:T(8,128)(2,1)}) fusion(bf16[32,128,1280]{2,1,0:T(8,128)(2,1)} %bitcast.58), kind=kLoop, calls=%fused_computation.113 | loop fusion | bytes 20971520 | tf_op jit(solution)/shard_map/slice | solution.py:64
  103.3 13.9 %fusion.17 = f32[10,128,4096]{2,1,0:T(8,128)} fusion(bf16[4096,640,1]{1,0,2:T(8,128)(2,1)} %bitcast.60, bf16[10,640]{1,0:T(8,128)(2,1)S(1)} %get-tuple-element.17, bf16[128,640]{1,0:T(8,128)(2,1)S(1)} %get-tuple-element.13), kind=kOutput, calls=%fused_computation.21 | convolution fusion | flops 6711705600 | bytes 26391040 | tf_op jit(solution)/shard_map/dot_general | solution.py:79
  117.3 21.3 %fusion.66 = f32[10,128]{1,0:T(8,128)S(1)} fusion(f32[10,128,4096]{2,1,0:T(8,128)} %fusion.17, pred[128,4096]{1,0:T(8,128)(4,1)S(1)} %fusion.14), kind=kOutput, calls=%fused_computation.114 | output fusion | flops 31461376 | bytes 21500928 | tf_op jit(solution)/shard_map/sub | solution.py:89
  138.6 25.4 %multiply_reduce_fusion = bf16[128,640]{1,0:T(8,128)(2,1)S(1)} fusion(bf16[4096,640,1]{1,0,2:T(8,128)(2,1)} %bitcast.59, f32[10,640]{1,0:T(8,128)S(1)} %get-tuple-element.18, f32[10,128]{1,0:T(8,128)S(1)} %fusion.66, f32[10,128,4096]{2,1,0:T(8,128)} %fusion.17, pred[128,4096]{1,0:T(8,128)(4,1)} %copy-done.5), kind=kOutput, calls=%fused_computation.11 | convolution fusion | flops 6744724480 | bytes 26933248 | tf_op jit(solution)/shard_map/dot_general | solution.py:91
  165.3 1.0 multiply_convert_fusion.2
  166.3 18.2 %all-gather.11.cloned.1.call-done = bf16[10304,125]{1,0:T(8,128)(2,1)} async-done(((bf16[1288,125]{1,0:T(8,128)(2,1)}), bf16[10304,125]{1,0:T(8,128)(2,1)}) %all-gather.11.cloned.1.call-update) | async-done | bytes 2576016 | tf_op jit(solution)/shard_map/all_gather | solution.py:63
  184.6 82.3 %all-gather.7.cloned.1.call-done = bf16[1024,1280]{1,0:T(8,128)(2,1)} async-done(((bf16[128,1280]{1,0:T(8,128)(2,1)}), bf16[1024,1280]{1,0:T(8,128)(2,1)}) %all-gather.7.cloned.1.call-update) | async-done | bytes 2621456 | tf_op jit(solution)/shard_map/all_gather | solution.py:103
  266.9 5.4 %fusion.67 = f32[1024,640]{1,0:T(8,128)} fusion(bf16[1024,1280]{1,0:T(8,128)(2,1)} %all-gather.7.cloned.1.call-done, bf16[1280,640]{1,0:T(8,128)(2,1)S(1)} %copy-done.11), kind=kOutput, calls=%fused_computation.115 | convolution fusion | flops 1677721600 | bytes 6881280 | tf_op jit(solution)/shard_map/dot_general | solution.py:104
  272.3 8.9 %convolution_convert_fusion = bf16[1024,1280]{1,0:T(8,128)(2,1)} fusion(bf16[640,1280]{1,0:T(8,128)(2,1)S(1)} %copy-done, f32[1024,640]{1,0:T(8,128)} %fusion.67, bf16[1024,1280]{1,0:T(8,128)(2,1)} %all-gather.7.cloned.1.call-done, bf16[1280,640]{1,0:T(8,128)(2,1)} %param.23, f32[640]{0:T(1024)S(1)} %copy-done.12, f32[640]{0:T(1024)S(1)} %copy-done.13), kind=kOutput, calls=%fused_computation.10 | convolution fusion | flops 3361996800 | bytes 11146240 | tf_op jit(solution)/shard_map/dot_general | solution.py:108
  282.4 95.8 %reduce-scatter.2.cloned.1.call-done = bf16[128,1280]{1,0:T(8,128)(2,1)} async-done(((bf16[1024,1280]{1,0:T(8,128)(2,1)}), bf16[128,1280]{1,0:T(8,128)(2,1)}) %reduce-scatter.2.cloned.1.call-update) | async-done | bytes 327696 | tf_op jit(solution)/shard_map/reduce_scatter | solution.py:107
  378.3 1.1 fusion.29
  379.4 1.3 multiply_reduce_fusion.1
  380.8 1.4 multiply_convert_fusion.1
  382.6 45.7 %all_gather.28 = bf16[32,8,1280]{2,1,0:T(8,128)(2,1)S(1)} all-gather(bf16[1,8,1280]{2,1,0:T(8,128)(2,1)S(1)} %pad_maximum_fusion.1), channel_id=1, replica_groups=mesh['dp'=8,'tensor'=32] {'tensor'}, dimensions={0}, use_global_device_ids=true | all-gather | bytes 675840 | tf_op jit(solution)/shard_map/all_gather | solution.py:129
  428.7 2.3 fusion.22
  431.2 73.0 %pmax.7 = f32[64]{0:T(128)S(1)} all-reduce(f32[64]{0:T(128)S(1)} %pad_maximum_fusion.2), channel_id=1, replica_groups=mesh['dp'=8,'tensor'=32] {'dp','tensor'}, use_global_device_ids=true, to_apply=%region_17.18 | all-reduce | flops 64 | bytes 512 | tf_op jit(solution)/shard_map/pmax | solution.py:151
  (82 shorter events, 8.0 us)
Async XLA Ops:
  7.2 265.2 %copy-start = (bf16[640,1280]{1,0:T(8,128)(2,1)S(1)}, bf16[640,1280]{1,0:T(8,128)(2,1)}, u32[]{:S(2)}) copy-start(bf16[640,1280]{1,0:T(8,128)(2,1)} %param.26) | copy-start | bytes 4915204
  7.2 86.3 %all-gather.9.cloned.1.call-start = ((), (), s32[]{:S(2)}) async-start(), calls=%async_computation.3 | async-start | bytes 10813440 | tf_op jit(solution)/shard_map/all_gather | solution.py:58
  11.9 3.3 copy-start.9
  13.9 3.2 copy-start.10
  14.8 5.4 %copy-start.8 = (s32[1,128]{1,0:T(1,128)S(1)}, s32[1,128]{1,0:T(1,128)}, u32[]{:S(2)}) copy-start(s32[1,128]{1,0:T(1,128)} %param.16) | copy-start | bytes 1540
  17.1 167.4 %all-gather.11.cloned.1.call-start = ((), (), s32[]{:S(2)}) async-start(), calls=%async_computation.4 | async-start | bytes 2967552 | tf_op jit(solution)/shard_map/all_gather | solution.py:63
  66.9 50.4 %copy-start.5 = (pred[128,4096]{1,0:T(8,128)(4,1)}, pred[128,4096]{1,0:T(8,128)(4,1)S(1)}, u32[]{:S(2)}) copy-start(pred[128,4096]{1,0:T(8,128)(4,1)S(1)} %fusion.14) | copy-start | bytes 1572868
  103.1 163.8 %all-gather.7.cloned.1.call-start = ((), (), s32[]{:S(2)}) async-start(), calls=%async_computation.1 | async-start | bytes 2949120 | tf_op jit(solution)/shard_map/all_gather | solution.py:103
  138.6 25.4 %copy-start.4 = (bf16[640,1280]{1,0:T(8,128)(2,1)S(1)}, bf16[640,1280]{1,0:T(8,128)(2,1)}, u32[]{:S(2)}) copy-start(bf16[640,1280]{1,0:T(8,128)(2,1)} %param.20) | copy-start | bytes 4915204
  138.6 25.9 %copy-start.6 = (f32[1280]{0:T(1024)S(1)}, f32[1280]{0:T(1024)}, u32[]{:S(2)}) copy-start(f32[1280]{0:T(1024)} %param.21) | copy-start | bytes 15364
  164.0 1.0 copy-start.1
  164.5 102.4 %copy-start.11 = (bf16[1280,640]{1,0:T(8,128)(2,1)S(1)}, bf16[1280,640]{1,0:T(8,128)(2,1)}, u32[]{:S(2)}) copy-start(bf16[1280,640]{1,0:T(8,128)(2,1)} %param.22) | copy-start | bytes 4915204
  184.5 87.8 %copy-start.12 = (f32[640]{0:T(1024)S(1)}, f32[640]{0:T(1024)}, u32[]{:S(2)}) copy-start(f32[640]{0:T(1024)} %param.25) | copy-start | bytes 7684
  184.5 87.8 %copy-start.13 = (f32[640]{0:T(1024)S(1)}, f32[640]{0:T(1024)}, u32[]{:S(2)}) copy-start(f32[640]{0:T(1024)} %param.24) | copy-start | bytes 7684
  184.5 193.7 %reduce-scatter.2.cloned.1.call-start = ((), (), s32[]{:S(2)}) async-start(), calls=%async_computation.2 | async-start | bytes 2949120 | tf_op jit(solution)/shard_map/reduce_scatter | solution.py:107
  281.3 98.2 %copy-start.2 = (bf16[128,1280]{1,0:T(8,128)(2,1)S(1)}, bf16[128,1280]{1,0:T(8,128)(2,1)}, u32[]{:S(2)}) copy-start(bf16[128,1280]{1,0:T(8,128)(2,1)} %multiply_convert_fusion.2) | copy-start | bytes 983044
  281.3 98.2 %copy-start.7 = (f32[1280]{0:T(1024)S(1)}, f32[1280]{0:T(1024)}, u32[]{:S(2)}) copy-start(f32[1280]{0:T(1024)} %param.27) | copy-start | bytes 15364
  382.1 123.5 %copy-start.3 = (bf16[128,1280]{1,0:T(8,128)(2,1)}, bf16[128,1280]{1,0:T(8,128)(2,1)S(1)}, u32[]{:S(2)}) copy-start(bf16[128,1280]{1,0:T(8,128)(2,1)S(1)} %multiply_convert_fusion.1) | copy-start | bytes 983044
  382.1 122.1 %copy-start.14 = (s32[32]{0:T(128)S(1)}, s32[32]{0:T(128)}, u32[]{:S(2)}) copy-start(s32[32]{0:T(128)} %param.17) | copy-start | bytes 388
Sparse Core Ops, SparseCore 0:
  17.2 76.2 all-gather.8
  103.2 81.2 all-gather.10
  187.7 79.1 all-gather.6
  281.4 96.8 reduce-scatter.1

commit v8 on v7

--- a/solution.py
+++ b/solution.py
@@ -122,8 +122,12 @@
     member = same_request.astype(jnp.float32)
     chosen = member * is_last[:, None].astype(jnp.float32)
     result_f32 = result_rows.astype(jnp.float32)
-    row_sums = jnp.dot(member.T, result_f32, precision=lax.Precision.HIGHEST)
-    last_rows = jnp.dot(chosen.T, result_f32, precision=lax.Precision.HIGHEST)
+    row_sums = jnp.dot(
+        member.T.astype(jnp.bfloat16), result_rows, preferred_element_type=jnp.float32
+    )
+    last_rows = jnp.dot(
+        chosen.T.astype(jnp.bfloat16), result_rows, preferred_element_type=jnp.float32
+    )
     partial = jnp.concatenate([row_sums, last_rows], axis=0)
     summed = jnp.sum(
         lax.all_gather(partial.astype(jnp.bfloat16), "tensor", axis=0, tiled=False).astype(

time: 513 us -> 513 us (level)
  no operation moved by 1% of the time
where the time goes in v8:
time: 513 us; the launch traced here: 512 us
  waiting for transfers between devices  223 us (43%)
  blocking collectives  165 us (32%)
  matrix products  61.7 us (12%)
  other arithmetic  32.6 us (6%)
  local copies, waits for them, and re-layouts  15.6 us (3%)
  between operations  14.1 us (3%)
    reduce_scatter x1, waiting for transfers between devices, local(): lax.psum_scatter(jnp.dot(hidden, w_down, preferred_element_type=jnp.float...  95.8 us
    all_gather x1, waiting for transfers between devices, local(): received = lax.all_gather(mid_rows, 'dp', axis=0, tiled=True)  82.3 us
    pmax x1, blocking collectives, local(): lax.pmax(jnp.concatenate([spread_max, spread_norm]), ('dp', 'tensor'))  73 us
    all_gather x1, blocking collectives, local(): seg_all = lax.all_gather(segments, 'tensor', axis=0, tiled=True)  46.1 us
    all_gather x1, blocking collectives, local(): lax.all_gather(partial.astype(jnp.bfloat16), 'tensor', axis=0, tiled=False)  45.7 us
    all_gather x1, waiting for transfers between devices, local(): gathered = lax.all_gather(packed, 'tensor', axis=0, tiled=False)  26.5 us
    dot_general x1, matrix products, local(): jnp.dot(weights.astype(jnp.bfloat16).reshape(HEADS * row_count, total_key...  25.4 us
    sub x1, other arithmetic, local(): scores - row_max[:, :, None]  21.3 us
  transfers between devices with their start and end apart: 4, of which 4 were waited for; matrix products, arithmetic and copies ran while one was open for 13% of the time, Pallas kernels for 0%

profile of v8, /device:TPU:1, one launch (start us, length us, event | category | flops | bytes accessed | tf_op | source)
XLA Modules:
  0.0 512.1 jit_solution(1264424142614423006)
XLA Ops:
  7.2 1.2 fusion.30
  8.5 3.4 fusion.62
  12.0 0.9 copy.26
  12.9 1.0 reduce_sum.118
  15.3 1.0 multiply_convert_fusion.4
  17.2 3.1 concatenate.24
  20.3 46.1 %all-gather = s32[1,4096]{1,0:T(1,128)S(1)} all-gather(s32[1,128]{1,0:T(1,128)S(1)} %copy-done.8), channel_id=2, replica_groups=mesh['dp'=8,'tensor'=32] {'tensor'}, dimensions={1}, use_global_device_ids=true | all-gather | bytes 16896 | tf_op jit(solution)/shard_map/all_gather | solution.py:66
  66.9 26.5 %all-gather.9.cloned.1.call-done = bf16[4096,1280]{1,0:T(8,128)(2,1)} async-done(((bf16[128,1280]{1,0:T(8,128)(2,1)}), bf16[4096,1280]{1,0:T(8,128)(2,1)}) %all-gather.9.cloned.1.call-update) | async-done | bytes 10485776 | tf_op jit(solution)/shard_map/all_gather | solution.py:58
  93.5 9.6 %fusion.64 = (bf16[32,128,640]{2,1,0:T(8,128)(2,1)}, bf16[32,128,640]{2,1,0:T(8,128)(2,1)}) fusion(bf16[32,128,1280]{2,1,0:T(8,128)(2,1)} %bitcast.58), kind=kLoop, calls=%fused_computation.115 | loop fusion | bytes 20971520 | tf_op jit(solution)/shard_map/slice | solution.py:64
  103.3 13.9 %fusion.17 = f32[10,128,4096]{2,1,0:T(8,128)} fusion(bf16[4096,640,1]{1,0,2:T(8,128)(2,1)} %bitcast.60, bf16[10,640]{1,0:T(8,128)(2,1)S(1)} %get-tuple-element.17, bf16[128,640]{1,0:T(8,128)(2,1)S(1)} %get-tuple-element.13), kind=kOutput, calls=%fused_computation.21 | convolution fusion | flops 6711705600 | bytes 26391040 | tf_op jit(solution)/shard_map/dot_general | solution.py:79
  117.3 21.3 %fusion.65 = f32[10,128]{1,0:T(8,128)S(1)} fusion(f32[10,128,4096]{2,1,0:T(8,128)} %fusion.17, pred[128,4096]{1,0:T(8,128)(4,1)S(1)} %fusion.14), kind=kOutput, calls=%fused_computation.116 | output fusion | flops 31461376 | bytes 21500928 | tf_op jit(solution)/shard_map/sub | solution.py:89
  138.6 25.4 %multiply_reduce_fusion = bf16[128,640]{1,0:T(8,128)(2,1)S(1)} fusion(bf16[4096,640,1]{1,0,2:T(8,128)(2,1)} %bitcast.59, f32[10,640]{1,0:T(8,128)S(1)} %get-tuple-element.18, f32[10,128]{1,0:T(8,128)S(1)} %fusion.65, f32[10,128,4096]{2,1,0:T(8,128)} %fusion.17, pred[128,4096]{1,0:T(8,128)(4,1)} %copy-done.5), kind=kOutput, calls=%fused_computation.11 | convolution fusion | flops 6744724480 | bytes 26933248 | tf_op jit(solution)/shard_map/dot_general | solution.py:91
  165.3 1.0 multiply_convert_fusion.2
  166.3 18.2 %all-gather.11.cloned.1.call-done = bf16[10304,125]{1,0:T(8,128)(2,1)} async-done(((bf16[1288,125]{1,0:T(8,128)(2,1)}), bf16[10304,125]{1,0:T(8,128)(2,1)}) %all-gather.11.cloned.1.call-update) | async-done | bytes 2576016 | tf_op jit(solution)/shard_map/all_gather | solution.py:63
  184.6 82.3 %all-gather.7.cloned.1.call-done = bf16[1024,1280]{1,0:T(8,128)(2,1)} async-done(((bf16[128,1280]{1,0:T(8,128)(2,1)}), bf16[1024,1280]{1,0:T(8,128)(2,1)}) %all-gather.7.cloned.1.call-update) | async-done | bytes 2621456 | tf_op jit(solution)/shard_map/all_gather | solution.py:103
  266.9 5.4 %fusion.66 = f32[1024,640]{1,0:T(8,128)} fusion(bf16[1024,1280]{1,0:T(8,128)(2,1)} %all-gather.7.cloned.1.call-done, bf16[1280,640]{1,0:T(8,128)(2,1)S(1)} %copy-done.11), kind=kOutput, calls=%fused_computation.117 | convolution fusion | flops 1677721600 | bytes 6881280 | tf_op jit(solution)/shard_map/dot_general | solution.py:104
  272.3 8.9 %convolution_convert_fusion = bf16[1024,1280]{1,0:T(8,128)(2,1)} fusion(bf16[640,1280]{1,0:T(8,128)(2,1)S(1)} %copy-done, f32[1024,640]{1,0:T(8,128)} %fusion.66, bf16[1024,1280]{1,0:T(8,128)(2,1)} %all-gather.7.cloned.1.call-done, bf16[1280,640]{1,0:T(8,128)(2,1)} %param.23, f32[640]{0:T(1024)S(1)} %copy-done.12, f32[640]{0:T(1024)S(1)} %copy-done.13), kind=kOutput, calls=%fused_computation.10 | convolution fusion | flops 3361996800 | bytes 11146240 | tf_op jit(solution)/shard_map/dot_general | solution.py:108
  282.4 95.8 %reduce-scatter.2.cloned.1.call-done = bf16[128,1280]{1,0:T(8,128)(2,1)} async-done(((bf16[1024,1280]{1,0:T(8,128)(2,1)}), bf16[128,1280]{1,0:T(8,128)(2,1)}) %reduce-scatter.2.cloned.1.call-update) | async-done | bytes 327696 | tf_op jit(solution)/shard_map/reduce_scatter | solution.py:107
  378.3 1.1 fusion.29
  379.4 1.3 multiply_reduce_fusion.1
  380.8 1.4 multiply_convert_fusion.1
  382.5 45.7 %all_gather.28 = bf16[32,8,1280]{2,1,0:T(8,128)(2,1)S(1)} all-gather(bf16[1,8,1280]{2,1,0:T(8,128)(2,1)S(1)} %pad_maximum_fusion.1), channel_id=1, replica_groups=mesh['dp'=8,'tensor'=32] {'tensor'}, dimensions={0}, use_global_device_ids=true | all-gather | bytes 675840 | tf_op jit(solution)/shard_map/all_gather | solution.py:133
  428.6 2.3 fusion.22
  431.1 73.0 %pmax.7 = f32[64]{0:T(128)S(1)} all-reduce(f32[64]{0:T(128)S(1)} %pad_maximum_fusion.2), channel_id=1, replica_groups=mesh['dp'=8,'tensor'=32] {'dp','tensor'}, use_global_device_ids=true, to_apply=%region_17.18 | all-reduce | flops 64 | bytes 512 | tf_op jit(solution)/shard_map/pmax | solution.py:155
  (82 shorter events, 7.9 us)
Async XLA Ops:
  7.2 265.2 %copy-start = (bf16[640,1280]{1,0:T(8,128)(2,1)S(1)}, bf16[640,1280]{1,0:T(8,128)(2,1)}, u32[]{:S(2)}) copy-start(bf16[640,1280]{1,0:T(8,128)(2,1)} %param.26) | copy-start | bytes 4915204
  7.2 86.3 %all-gather.9.cloned.1.call-start = ((), (), s32[]{:S(2)}) async-start(), calls=%async_computation.3 | async-start | bytes 10813440 | tf_op jit(solution)/shard_map/all_gather | solution.py:58
  11.9 3.3 copy-start.9
  13.9 3.2 copy-start.10
  14.8 5.4 %copy-start.8 = (s32[1,128]{1,0:T(1,128)S(1)}, s32[1,128]{1,0:T(1,128)}, u32[]{:S(2)}) copy-start(s32[1,128]{1,0:T(1,128)} %param.16) | copy-start | bytes 1540
  17.1 167.4 %all-gather.11.cloned.1.call-start = ((), (), s32[]{:S(2)}) async-start(), calls=%async_computation.4 | async-start | bytes 2967552 | tf_op jit(solution)/shard_map/all_gather | solution.py:63
  66.9 50.4 %copy-start.5 = (pred[128,4096]{1,0:T(8,128)(4,1)}, pred[128,4096]{1,0:T(8,128)(4,1)S(1)}, u32[]{:S(2)}) copy-start(pred[128,4096]{1,0:T(8,128)(4,1)S(1)} %fusion.14) | copy-start | bytes 1572868
  103.1 163.8 %all-gather.7.cloned.1.call-start = ((), (), s32[]{:S(2)}) async-start(), calls=%async_computation.1 | async-start | bytes 2949120 | tf_op jit(solution)/shard_map/all_gather | solution.py:103
  138.6 25.4 %copy-start.4 = (bf16[640,1280]{1,0:T(8,128)(2,1)S(1)}, bf16[640,1280]{1,0:T(8,128)(2,1)}, u32[]{:S(2)}) copy-start(bf16[640,1280]{1,0:T(8,128)(2,1)} %param.20) | copy-start | bytes 4915204
  138.6 25.9 %copy-start.6 = (f32[1280]{0:T(1024)S(1)}, f32[1280]{0:T(1024)}, u32[]{:S(2)}) copy-start(f32[1280]{0:T(1024)} %param.21) | copy-start | bytes 15364
  164.0 1.0 copy-start.1
  164.5 102.4 %copy-start.11 = (bf16[1280,640]{1,0:T(8,128)(2,1)S(1)}, bf16[1280,640]{1,0:T(8,128)(2,1)}, u32[]{:S(2)}) copy-start(bf16[1280,640]{1,0:T(8,128)(2,1)} %param.22) | copy-start | bytes 4915204
  184.5 87.8 %copy-start.12 = (f32[640]{0:T(1024)S(1)}, f32[640]{0:T(1024)}, u32[]{:S(2)}) copy-start(f32[640]{0:T(1024)} %param.25) | copy-start | bytes 7684
  184.5 87.8 %copy-start.13 = (f32[640]{0:T(1024)S(1)}, f32[640]{0:T(1024)}, u32[]{:S(2)}) copy-start(f32[640]{0:T(1024)} %param.24) | copy-start | bytes 7684
  184.5 193.7 %reduce-scatter.2.cloned.1.call-start = ((), (), s32[]{:S(2)}) async-start(), calls=%async_computation.2 | async-start | bytes 2949120 | tf_op jit(solution)/shard_map/reduce_scatter | solution.py:107
  281.3 98.2 %copy-start.2 = (bf16[128,1280]{1,0:T(8,128)(2,1)S(1)}, bf16[128,1280]{1,0:T(8,128)(2,1)}, u32[]{:S(2)}) copy-start(bf16[128,1280]{1,0:T(8,128)(2,1)} %multiply_convert_fusion.2) | copy-start | bytes 983044
  281.3 98.2 %copy-start.7 = (f32[1280]{0:T(1024)S(1)}, f32[1280]{0:T(1024)}, u32[]{:S(2)}) copy-start(f32[1280]{0:T(1024)} %param.27) | copy-start | bytes 15364
  382.1 123.4 %copy-start.3 = (bf16[128,1280]{1,0:T(8,128)(2,1)}, bf16[128,1280]{1,0:T(8,128)(2,1)S(1)}, u32[]{:S(2)}) copy-start(bf16[128,1280]{1,0:T(8,128)(2,1)S(1)} %multiply_convert_fusion.1) | copy-start | bytes 983044
  382.1 122.0 %copy-start.14 = (s32[32]{0:T(128)S(1)}, s32[32]{0:T(128)}, u32[]{:S(2)}) copy-start(s32[32]{0:T(128)} %param.17) | copy-start | bytes 388
Sparse Core Ops, SparseCore 0:
  17.2 76.2 all-gather.8
  103.2 81.2 all-gather.10
  187.7 79.1 all-gather.6
  281.4 96.8 reduce-scatter.1
